TPU v7x, 128 devices: a whole 4x4x4 slice. The times are simulated.
128 devices in a mesh: segment: 2 (over core), tensor: 4 (over x), batch: 16 (over z, y).
Axes of the slice: x: 4, y: 4, z: 4, core: 2. Of those that a mesh axis runs over, the one named last changes fastest.
Arguments:
- hidden: bfloat16 [3, 128, 16384], P(None, 'tensor', 'batch'), may hold values from -6 to 6
- norm_gain: bfloat16 [2, 16384], P('segment', 'batch'), may hold values from 0.25 to 1.75
- w_query: bfloat16 [2, 16384, 8192], P('segment', 'batch', 'tensor'), may hold values from -0.046875 to 0.046875
- key_value_weight: bfloat16 [2, 16384, 2048], P('segment', 'batch', 'tensor'), may hold values from -0.046875 to 0.046875
- w_out: bfloat16 [2, 8192, 16384], P('segment', 'tensor', 'batch'), may hold values from -0.0625 to 0.0625
- key_value_cache: bfloat16 [2, 32, 8, 256, 256], P('segment', 'batch', 'tensor'), may hold values from -6 to 6
- owner_slot: int32 [32], replicated, may hold values from 0 to 31, each once
- accepted: int32 [3, 32], replicated, may hold values from 1 to 4
Outputs:
- layer_outputs: bfloat16 [2, 3, 128, 16384], P('segment', None, 'tensor', 'batch')
- new_cache: bfloat16 [2, 32, 8, 12, 256], P('segment', 'batch', 'tensor')
Inputs may be any that keep to these rules, and one draw needn't show every extreme that they name: `owner_slot`: each slot is held by exactly one request; slot s belongs to index s // 2 of batch.
All inputs are finite; a program needn't handle non-finite values.
Results may differ from a plain program's by a relative error of at most 0.0095.
Values may be sent and summed in bfloat16 or wider, within the bound.
No kernel may reach another device: no remote copies, remote signals or barrier semaphores. Data moves between devices by JAX's collectives and lax.ppermute only.
A program may use at most 64 MiB of HBM per device.

v0:
```python
import jax
import jax.numpy as jnp
from jax import lax
from jax.sharding import PartitionSpec as P

MODEL_WIDTH = 16384
HEAD_SIZE = 128
DRAFT_BLOCK = 4
DECODE_ROUNDS = 3
GROUP_HEADS = 8


def passed_along(block, axis, distance):
    devices = range(lax.axis_size(axis))
    route = [(i - distance, i) for i in devices if i - distance in devices]
    return lax.ppermute(block, axis, route)


def pass_on(rows):
    return passed_along(rows, "segment", 1)


def shards(
    hidden, norm_gain, w_query, key_value_weight, w_out, key_value_cache, owner_slot, accepted
):
    n_segment = lax.axis_size("segment")
    segment = lax.axis_index("segment")
    group = lax.axis_index("batch")
    requests = owner_slot.shape[0]
    slots = key_value_cache.shape[1]
    kv_local = key_value_cache.shape[2]
    query_cols = w_query.shape[2]
    own_rows = slots * DRAFT_BLOCK
    scale = HEAD_SIZE ** (-0.5)
    gain = norm_gain[0].astype(jnp.float32)
    cache_local = key_value_cache[0]
    onehot = (owner_slot[None, :] == jnp.arange(requests)[:, None]).astype(jnp.int32)
    inverse = jnp.sum(onehot * jnp.arange(requests)[None, :], axis=1)
    acc_slot = jnp.sum(onehot[None] * accepted[:, None, :], axis=2)
    acc_own = lax.dynamic_slice_in_dim(acc_slot, group * slots, slots, 1)
    sort_index = (inverse[:, None] * DRAFT_BLOCK + jnp.arange(DRAFT_BLOCK)[None, :]).reshape(-1)
    back_index = (owner_slot[:, None] * DRAFT_BLOCK + jnp.arange(DRAFT_BLOCK)[None, :]).reshape(-1)
    positions = jnp.arange(DECODE_ROUNDS * DRAFT_BLOCK)
    round_of = positions // DRAFT_BLOCK
    place = positions % DRAFT_BLOCK
    causal = jnp.arange(DRAFT_BLOCK)[None, :] <= jnp.arange(DRAFT_BLOCK)[:, None]
    ext = jnp.zeros((slots, kv_local, DECODE_ROUNDS * DRAFT_BLOCK, 2 * HEAD_SIZE), jnp.bfloat16)
    record = jnp.zeros((DECODE_ROUNDS,) + hidden.shape[1:], jnp.bfloat16)
    x = jnp.zeros(hidden.shape[1:], jnp.bfloat16)
    for rnd in range(DECODE_ROUNDS):
        for step in range(n_segment):
            if step == 0:
                x = jnp.where(segment == 0, hidden[rnd], x)
            layer_rnd = jnp.int32(rnd)
            xf = x.astype(jnp.float32)
            total = lax.psum(jnp.sum(xf * xf, axis=1), "batch")
            normed = (xf * lax.rsqrt(total / MODEL_WIDTH + 1e-05)[:, None] * gain[None, :]).astype(
                jnp.bfloat16
            )
            rows_all = lax.all_gather(normed, "tensor", axis=0, tiled=True)
            sorted_rows = jnp.take(rows_all, sort_index, axis=0)
            first = jnp.dot(sorted_rows, w_query[0], preferred_element_type=jnp.float32)
            second = jnp.dot(sorted_rows, key_value_weight[0], preferred_element_type=jnp.float32)
            proj = lax.psum_scatter(
                jnp.concatenate([first, second], axis=1), "batch", scatter_dimension=0, tiled=True
            )
            query_rows_new = proj[:, :query_cols].astype(jnp.bfloat16)
            key_value_rows = proj[:, query_cols:].astype(jnp.bfloat16)
            query_heads = query_rows_new.reshape(
                slots, DRAFT_BLOCK, kv_local, GROUP_HEADS, HEAD_SIZE
            )
            fresh_key_value = key_value_rows.reshape(
                slots, DRAFT_BLOCK, kv_local, 2 * HEAD_SIZE
            ).transpose(0, 2, 1, 3)
            keys_all = jnp.concatenate([cache_local, ext, fresh_key_value], axis=2)
            acc_by_pos = acc_own[round_of, :].T
            ext_valid = (round_of[None, :] < layer_rnd) & (place[None, :] < acc_by_pos)
            mask = jnp.concatenate(
                [
                    jnp.ones((slots, DRAFT_BLOCK, cache_local.shape[2]), bool),
                    jnp.broadcast_to(
                        ext_valid[:, None, :], (slots, DRAFT_BLOCK, DECODE_ROUNDS * DRAFT_BLOCK)
                    ),
                    jnp.broadcast_to(causal[None], (slots, DRAFT_BLOCK, DRAFT_BLOCK)),
                ],
                axis=2,
            )
            scores = (
                jnp.einsum(
                    "sjhgd,shld->shgjl",
                    query_heads,
                    keys_all[..., :HEAD_SIZE],
                    preferred_element_type=jnp.float32,
                )
                * scale
            )
            scores = jnp.where(mask[:, None, None], scores, -1e30)
            weights = jax.nn.softmax(scores, axis=-1).astype(jnp.bfloat16)
            attended = jnp.einsum(
                "shgjl,shld->sjhgd",
                weights,
                keys_all[..., HEAD_SIZE:],
                preferred_element_type=jnp.float32,
            )
            attended = attended.astype(jnp.bfloat16).reshape(own_rows, query_cols)
            partial_out = jnp.dot(
                lax.all_gather(attended, "batch", axis=0, tiled=True),
                w_out[0],
                preferred_element_type=jnp.float32,
            )
            unsorted = jnp.take(partial_out, back_index, axis=0)
            summed = lax.psum_scatter(
                unsorted.astype(jnp.bfloat16), "tensor", scatter_dimension=0, tiled=True
            ).astype(jnp.float32)
            x_new = (xf + summed).astype(jnp.bfloat16)
            acc_now = lax.dynamic_index_in_dim(acc_own, layer_rnd, 0, keepdims=False)
            keep = jnp.arange(DRAFT_BLOCK)[None, :] < acc_now[:, None]
            masked = jnp.where(
                keep[:, None, :, None], fresh_key_value, jnp.zeros_like(fresh_key_value)
            )
            ext_new = lax.dynamic_update_slice(ext, masked, (0, 0, layer_rnd * DRAFT_BLOCK, 0))
            x_new, ext_new = (x_new, ext_new)
            active = segment == step
            ext = jnp.where(active, ext_new, ext)
            record = record.at[rnd].set(jnp.where(active, x_new, record[rnd]))
            if step + 1 < n_segment:
                x = pass_on(x_new)
    return (record[None], ext[None])


def solution(mesh):
    in_specs = (
        P(None, "tensor", "batch"),
        P("segment", "batch"),
        P("segment", "batch", "tensor"),
        P("segment", "batch", "tensor"),
        P("segment", "tensor", "batch"),
        P("segment", "batch", "tensor", None, None),
        P(),
        P(),
    )
    out_specs = (P("segment", None, "tensor", "batch"), P("segment", "batch", "tensor", None, None))
    return jax.shard_map(shards, mesh=mesh, in_specs=in_specs, out_specs=out_specs, check_vma=False)
```

profile of v0, /device:TPU:0, one launch (start us, length us, event | category | flops | bytes accessed | tf_op | source)
XLA Modules:
  0.0 944.5 jit_solution(7901623505001223784)
XLA Ops:
  14.7 42.0 %psum.42 = f32[32]{0:T(128)S(1)} all-reduce(f32[32]{0:T(128)S(1)} %fusion.92), channel_id=1, replica_groups=mesh['segment'=2,'tensor'=4,'batch'=16] {'batch'}, use_global_device_ids=true, to_apply=%region_1.0 | all-reduce | flops 32 | bytes 256 | tf_op jit(solution)/shard_map/psum | solution.py:56
  57.7 12.6 %all_gather.36 = bf16[128,1024]{1,0:T(8,128)(2,1)S(1)} all-gather(bf16[32,1024]{1,0:T(8,128)(2,1)S(1)} %fusion.94), channel_id=1, replica_groups=mesh['segment'=2,'tensor'=4,'batch'=16] {'tensor'}, dimensions={0}, use_global_device_ids=true | all-gather | bytes 327680 | tf_op jit(solution)/shard_map/all_gather | solution.py:60
  74.6 82.2 %all-reduce.16 = bf16[128,2560]{1,0:T(8,128)(2,1)S(1)} all-reduce(f32[128,2560]{1,0:T(8,128)S(1)} %pad_maximum_fusion), channel_id=2, replica_groups=mesh['segment'=2,'tensor'=4,'batch'=16] {'batch'}, use_global_device_ids=true, to_apply=%region_3.5.clone | all-reduce | flops 327680 | bytes 1966080
  164.6 20.9 %all_gather.37 = bf16[128,2048]{1,0:T(8,128)(2,1)S(1)} all-gather(bf16[8,2048]{1,0:T(8,128)(2,1)S(1)} %reshape.476), channel_id=1, replica_groups=mesh['segment'=2,'tensor'=4,'batch'=16] {'batch'}, dimensions={0}, use_global_device_ids=true | all-gather | bytes 557056 | tf_op jit(solution)/shard_map/all_gather | solution.py:107
  190.5 20.0 %reduce-scatter.7.cloned.1.call-done = bf16[32,1024]{1,0:T(8,128)(2,1)} async-done(((bf16[128,1024]{1,0:T(8,128)(2,1)}), bf16[32,1024]{1,0:T(8,128)(2,1)}) %reduce-scatter.7.cloned.1.call-update) | async-done | bytes 65552 | tf_op jit(solution)/shard_map/reduce_scatter | solution.py:112
  213.6 40.6 %all-reduce.11 = (f32[32]{0:T(128)S(1)}, f32[32]{0:T(128)S(1)}) all-reduce(f32[32]{0:T(128)S(1)} %get-tuple-element.111, f32[32]{0:T(128)S(1)} %get-tuple-element.102), channel_id=1, replica_groups=mesh['segment'=2,'tensor'=4,'batch'=16] {'batch'}, use_global_device_ids=true, to_apply=%region_9.12 | all-reduce | flops 64 | bytes 512 | tf_op jit(solution)/shard_map/psum | solution.py:56
  254.3 12.4 %all_gather.38 = bf16[128,1024]{1,0:T(8,128)(2,1)S(1)} all-gather(bf16[32,1024]{1,0:T(8,128)(2,1)S(1)} %get-tuple-element.115), channel_id=1, replica_groups=mesh['segment'=2,'tensor'=4,'batch'=16] {'tensor'}, dimensions={0}, use_global_device_ids=true | all-gather | bytes 327680 | tf_op jit(solution)/shard_map/all_gather | solution.py:60
  289.7 88.6 %all-reduce.17 = (bf16[128,2560]{1,0:T(8,128)(2,1)}, bf16[128,2560]{1,0:T(8,128)(2,1)}) all-reduce(f32[128,2560]{1,0:T(8,128)S(1)} %pad_maximum_fusion.1, f32[128,2560]{1,0:T(8,128)} %pad_maximum_fusion.2), channel_id=4, replica_groups=mesh['segment'=2,'tensor'=4,'batch'=16] {'batch'}, use_global_device_ids=true, to_apply=%region_10.13.clone | all-reduce | flops 655360 | bytes 3932160
  382.7 21.0 %all_gather.41 = bf16[128,2048]{1,0:T(8,128)(2,1)S(1)} all-gather(bf16[8,2048]{1,0:T(8,128)(2,1)S(1)} %reshape.483), channel_id=1, replica_groups=mesh['segment'=2,'tensor'=4,'batch'=16] {'batch'}, dimensions={0}, use_global_device_ids=true | all-gather | bytes 557056 | tf_op jit(solution)/shard_map/all_gather | solution.py:107
  408.3 24.3 %all_gather.39 = bf16[128,2048]{1,0:T(8,128)(2,1)S(1)} all-gather(bf16[8,2048]{1,0:T(8,128)(2,1)S(1)} %reshape.479), channel_id=1, replica_groups=mesh['segment'=2,'tensor'=4,'batch'=16] {'batch'}, dimensions={0}, use_global_device_ids=true | all-gather | bytes 557056 | tf_op jit(solution)/shard_map/all_gather | solution.py:107
  438.8 16.3 %reduce-scatter.9.cloned.1.call-done = bf16[32,1024]{1,0:T(8,128)(2,1)} async-done(((bf16[128,1024]{1,0:T(8,128)(2,1)}), bf16[32,1024]{1,0:T(8,128)(2,1)}) %reduce-scatter.9.cloned.1.call-update) | async-done | bytes 65552 | tf_op jit(solution)/shard_map/reduce_scatter | solution.py:112
  456.0 22.1 %reduce-scatter.11.cloned.1.call-done = bf16[32,1024]{1,0:T(8,128)(2,1)} async-done(((bf16[128,1024]{1,0:T(8,128)(2,1)}), bf16[32,1024]{1,0:T(8,128)(2,1)}) %reduce-scatter.11.cloned.1.call-update) | async-done | bytes 65552 | tf_op jit(solution)/shard_map/reduce_scatter | solution.py:112
  482.1 40.6 %all-reduce.9 = (f32[32]{0:T(128)S(1)}, f32[32]{0:T(128)S(1)}) all-reduce(f32[32]{0:T(128)S(1)} %get-tuple-element.110, f32[32]{0:T(128)S(1)} %get-tuple-element.98), channel_id=1, replica_groups=mesh['segment'=2,'tensor'=4,'batch'=16] {'batch'}, use_global_device_ids=true, to_apply=%region_21.24 | all-reduce | flops 64 | bytes 512 | tf_op jit(solution)/shard_map/psum | solution.py:56
  522.9 12.3 %all_gather.42 = bf16[128,1024]{1,0:T(8,128)(2,1)S(1)} all-gather(bf16[32,1024]{1,0:T(8,128)(2,1)S(1)} %get-tuple-element.113), channel_id=1, replica_groups=mesh['segment'=2,'tensor'=4,'batch'=16] {'tensor'}, dimensions={0}, use_global_device_ids=true | all-gather | bytes 327680 | tf_op jit(solution)/shard_map/all_gather | solution.py:60
  558.3 88.6 %all-reduce.18 = (bf16[128,2560]{1,0:T(8,128)(2,1)}, bf16[128,2560]{1,0:T(8,128)(2,1)}) all-reduce(f32[128,2560]{1,0:T(8,128)S(1)} %pad_maximum_fusion.3, f32[128,2560]{1,0:T(8,128)} %pad_maximum_fusion.4), channel_id=8, replica_groups=mesh['segment'=2,'tensor'=4,'batch'=16] {'batch'}, use_global_device_ids=true, to_apply=%region_22.25.clone | all-reduce | flops 655360 | bytes 3932160
  651.4 21.0 %all_gather.45 = bf16[128,2048]{1,0:T(8,128)(2,1)S(1)} all-gather(bf16[8,2048]{1,0:T(8,128)(2,1)S(1)} %reshape.490), channel_id=1, replica_groups=mesh['segment'=2,'tensor'=4,'batch'=16] {'batch'}, dimensions={0}, use_global_device_ids=true | all-gather | bytes 557056 | tf_op jit(solution)/shard_map/all_gather | solution.py:107
  677.1 24.1 %all_gather.43 = bf16[128,2048]{1,0:T(8,128)(2,1)S(1)} all-gather(bf16[8,2048]{1,0:T(8,128)(2,1)S(1)} %reshape.486), channel_id=1, replica_groups=mesh['segment'=2,'tensor'=4,'batch'=16] {'batch'}, dimensions={0}, use_global_device_ids=true | all-gather | bytes 557056 | tf_op jit(solution)/shard_map/all_gather | solution.py:107
  706.8 17.1 %reduce-scatter.13.cloned.1.call-done = bf16[32,1024]{1,0:T(8,128)(2,1)} async-done(((bf16[128,1024]{1,0:T(8,128)(2,1)}), bf16[32,1024]{1,0:T(8,128)(2,1)}) %reduce-scatter.13.cloned.1.call-update) | async-done | bytes 65552 | tf_op jit(solution)/shard_map/reduce_scatter | solution.py:112
  724.9 21.9 %reduce-scatter.15.cloned.1.call-done = bf16[32,1024]{1,0:T(8,128)(2,1)} async-done(((bf16[128,1024]{1,0:T(8,128)(2,1)}), bf16[32,1024]{1,0:T(8,128)(2,1)}) %reduce-scatter.15.cloned.1.call-update) | async-done | bytes 65552 | tf_op jit(solution)/shard_map/reduce_scatter | solution.py:112
  749.9 40.5 %psum.47 = f32[32]{0:T(128)S(1)} all-reduce(f32[32]{0:T(128)S(1)} %fusion.88), channel_id=1, replica_groups=mesh['segment'=2,'tensor'=4,'batch'=16] {'batch'}, use_global_device_ids=true, to_apply=%region_33.36 | all-reduce | flops 32 | bytes 256 | tf_op jit(solution)/shard_map/psum | solution.py:56
  790.6 12.3 %all_gather.46 = bf16[128,1024]{1,0:T(8,128)(2,1)S(1)} all-gather(bf16[32,1024]{1,0:T(8,128)(2,1)S(1)} %fusion.90), channel_id=1, replica_groups=mesh['segment'=2,'tensor'=4,'batch'=16] {'tensor'}, dimensions={0}, use_global_device_ids=true | all-gather | bytes 327680 | tf_op jit(solution)/shard_map/all_gather | solution.py:60
  807.3 82.3 %all-reduce.19 = bf16[128,2560]{1,0:T(8,128)(2,1)} all-reduce(f32[128,2560]{1,0:T(8,128)S(1)} %pad_maximum_fusion.5), channel_id=12, replica_groups=mesh['segment'=2,'tensor'=4,'batch'=16] {'batch'}, use_global_device_ids=true, to_apply=%region_34.37.clone | all-reduce | flops 327680 | bytes 1966080
  891.2 20.9 %all_gather.47 = bf16[128,2048]{1,0:T(8,128)(2,1)S(1)} all-gather(bf16[8,2048]{1,0:T(8,128)(2,1)S(1)} %reshape.493), channel_id=1, replica_groups=mesh['segment'=2,'tensor'=4,'batch'=16] {'batch'}, dimensions={0}, use_global_device_ids=true | all-gather | bytes 557056 | tf_op jit(solution)/shard_map/all_gather | solution.py:107
  917.7 18.5 %reduce-scatter.17.cloned.1.call-done = bf16[32,1024]{1,0:T(8,128)(2,1)} async-done(((bf16[128,1024]{1,0:T(8,128)(2,1)}), bf16[32,1024]{1,0:T(8,128)(2,1)}) %reduce-scatter.17.cloned.1.call-update) | async-done | bytes 65552 | tf_op jit(solution)/shard_map/reduce_scatter | solution.py:112
  (258 shorter events, 125.7 us)
Async XLA Ops:
  7.2 64.0 %copy-start = (bf16[1,1024,512]{2,1,0:T(8,128)(2,1)S(1)}, bf16[1,1024,512]{2,1,0:T(8,128)(2,1)}, u32[]{:S(2)}) copy-start(bf16[1,1024,512]{2,1,0:T(8,128)(2,1)} %param.27) | copy-start | bytes 3145732
  7.2 203.3 %reduce-scatter.7.cloned.1.call-start = ((), (), s32[]{:S(2)}) async-start(), calls=%async_computation.6 | async-start | bytes 327680 | tf_op jit(solution)/shard_map/reduce_scatter | solution.py:112
  70.3 213.8 %copy-start.16 = (s32[1024]{0:T(1024)}, s32[1024]{0:T(1024)S(1)}, u32[]{:S(2)}) copy-start(s32[1024]{0:T(1024)S(1)} %pad_clamp_fusion.2) | copy-start | bytes 12292
  74.6 88.5 %copy-start.1 = (bf16[1,2,2,256,256]{4,3,2,1,0:T(8,128)(2,1)S(1)}, bf16[1,2,2,256,256]{4,3,2,1,0:T(8,128)(2,1)}, u32[]{:S(2)}) copy-start(bf16[1,2,2,256,256]{4,3,2,1,0:T(8,128)(2,1)} %param.29) | copy-start | bytes 1572868
  158.9 277.4 %copy-start.18 = (pred[128]{0:T(512)(128)(4,1)}, pred[128]{0:T(512)(128)(4,1)S(1)}, u32[]{:S(2)}) copy-start(pred[128]{0:T(512)(128)(4,1)S(1)} %compare_and_fusion) | copy-start | bytes 388
  163.8 216.3 %copy-start.24 = (pred[2,4,272]{2,1,0:T(4,128)(4,1)}, pred[2,4,272]{2,1,0:T(4,128)(4,1)S(1)}, u32[]{:S(2)}) copy-start(pred[2,4,272]{2,1,0:T(4,128)(4,1)S(1)} %get-tuple-element.122) | copy-start | bytes 6532
  185.6 249.9 %copy-start.17 = (s32[1024]{0:T(1024)}, s32[1024]{0:T(1024)S(1)}, u32[]{:S(2)}) copy-start(s32[1024]{0:T(1024)S(1)} %pad_clamp_fusion) | copy-start | bytes 12292
  190.2 264.9 %reduce-scatter.9.cloned.1.call-start = ((), (), s32[]{:S(2)}) async-start(), calls=%async_computation.7 | async-start | bytes 327680 | tf_op jit(solution)/shard_map/reduce_scatter | solution.py:112
  211.3 2.2 collective-permute-start
  212.6 54.9 %copy-start.7 = (bf16[2,2,12,256]{3,2,1,0:T(8,128)(2,1)}, bf16[2,2,12,256]{3,2,1,0:T(8,128)(2,1)S(1)}, u32[]{:S(2)}) copy-start(bf16[2,2,12,256]{3,2,1,0:T(8,128)(2,1)S(1)} %pad_select_fusion) | copy-start | bytes 73732
  289.7 90.3 %copy-start.11 = (bf16[2,2,12,256]{3,2,1,0:T(8,128)(2,1)S(1)}, bf16[2,2,12,256]{3,2,1,0:T(8,128)(2,1)}, u32[]{:S(2)}) copy-start(bf16[2,2,12,256]{3,2,1,0:T(8,128)(2,1)} %copy-done.7) | copy-start | bytes 73732
  289.7 90.4 %copy-start.8 = (bf16[2,2,12,256]{3,2,1,0:T(8,128)(2,1)S(1)}, bf16[2,2,12,256]{3,2,1,0:T(8,128)(2,1)}, u32[]{:S(2)}) copy-start(bf16[2,2,12,256]{3,2,1,0:T(8,128)(2,1)} %copy-done.7) | copy-start | bytes 73732
  380.0 58.8 %copy-start.9 = (bf16[2,2,12,256]{3,2,1,0:T(8,128)(2,1)}, bf16[2,2,12,256]{3,2,1,0:T(8,128)(2,1)S(1)}, u32[]{:S(2)}) copy-start(bf16[2,2,12,256]{3,2,1,0:T(8,128)(2,1)S(1)} %fusion.121) | copy-start | bytes 73732
  437.3 40.8 %reduce-scatter.11.cloned.1.call-start = ((), (), s32[]{:S(2)}) async-start(), calls=%async_computation.8 | async-start | bytes 327680 | tf_op jit(solution)/shard_map/reduce_scatter | solution.py:112
  438.1 285.9 %reduce-scatter.13.cloned.1.call-start = ((), (), s32[]{:S(2)}) async-start(), calls=%async_computation.9 | async-start | bytes 327680 | tf_op jit(solution)/shard_map/reduce_scatter | solution.py:112
  438.8 96.3 %copy-start.21 = (pred[2,4]{1,0:T(4,128)(4,1)}, pred[2,4]{1,0:T(4,128)(4,1)S(1)}, u32[]{:S(2)}) copy-start(pred[2,4]{1,0:T(4,128)(4,1)S(1)} %get-tuple-element.133) | copy-start | bytes 28
  479.0 2.2 collective-permute-start.1
  558.3 90.3 %copy-start.10 = (bf16[2,2,12,256]{3,2,1,0:T(8,128)(2,1)S(1)}, bf16[2,2,12,256]{3,2,1,0:T(8,128)(2,1)}, u32[]{:S(2)}) copy-start(bf16[2,2,12,256]{3,2,1,0:T(8,128)(2,1)} %copy-done.9) | copy-start | bytes 73732
  558.3 90.3 %copy-start.12 = (bf16[2,2,12,256]{3,2,1,0:T(8,128)(2,1)S(1)}, bf16[2,2,12,256]{3,2,1,0:T(8,128)(2,1)}, u32[]{:S(2)}) copy-start(bf16[2,2,12,256]{3,2,1,0:T(8,128)(2,1)} %copy.173) | copy-start | bytes 73732
  558.3 90.3 %copy-start.22 = (pred[2,4]{1,0:T(4,128)(4,1)S(1)}, pred[2,4]{1,0:T(4,128)(4,1)}, u32[]{:S(2)}) copy-start(pred[2,4]{1,0:T(4,128)(4,1)} %copy-done.21) | copy-start | bytes 28
  558.3 90.4 %copy-start.14 = (bf16[2,2,12,256]{3,2,1,0:T(8,128)(2,1)S(1)}, bf16[2,2,12,256]{3,2,1,0:T(8,128)(2,1)}, u32[]{:S(2)}) copy-start(bf16[2,2,12,256]{3,2,1,0:T(8,128)(2,1)} %copy-done.13) | copy-start | bytes 73732
  706.2 40.6 %reduce-scatter.15.cloned.1.call-start = ((), (), s32[]{:S(2)}) async-start(), calls=%async_computation.10 | async-start | bytes 327680 | tf_op jit(solution)/shard_map/reduce_scatter | solution.py:112
  706.8 229.4 %reduce-scatter.17.cloned.1.call-start = ((), (), s32[]{:S(2)}) async-start(), calls=%async_computation.11 | async-start | bytes 327680 | tf_op jit(solution)/shard_map/reduce_scatter | solution.py:112
  747.6 2.2 collective-permute-start.2
  (12 other events, 182.0 us)
Sparse Core Ops, SparseCore 0:
  190.4 20.0 reduce-scatter.6
  437.5 17.6 reduce-scatter.8
  457.5 20.5 reduce-scatter.10
  706.3 17.6 reduce-scatter.12
  726.2 20.5 reduce-scatter.14
  917.1 19.0 reduce-scatter.16
where the time goes:
time: 947 us; the launch traced here: 945 us
  blocking collectives  712 us (75%)
  waiting for transfers between devices  119 us (13%)
  matrix products  44.8 us (5%)
  other arithmetic  28.4 us (3%)
  local copies, waits for them, and re-layouts  20.8 us (2%)
  between operations  15.8 us (2%)
    unnamed x4, blocking collectives  342 us
    psum x4, blocking collectives, shards(): total = lax.psum(jnp.sum(xf * xf, axis=1), 'batch')  164 us
    all_gather x6, blocking collectives, shards(): lax.all_gather(attended, 'batch', axis=0, tiled=True)  132 us
    reduce_scatter x6, waiting for transfers between devices, shards(): lax.psum_scatter(unsorted.astype(jnp.bfloat16), 'tensor', scatter_dimensi...  116 us
    all_gather x6, blocking collectives, shards(): rows_all = lax.all_gather(normed, 'tensor', axis=0, tiled=True)  74 us
    dot_general x6, matrix products, shards(): first = jnp.dot(sorted_rows, w_query[0], preferred_element_type=jnp.float32)  19.9 us
  transfers between devices with their start and end apart: 9, of which 9 were waited for; matrix products, arithmetic and copies ran while one was open for 0% of the time, Pallas kernels for 0%

commit v1 on v0

v1 whole, which is shorter than its diff:
```python
import jax
import jax.numpy as jnp
from jax import lax
from jax.sharding import PartitionSpec as P

MODEL_WIDTH = 16384
HEAD_SIZE = 128
DRAFT_BLOCK = 4
DECODE_ROUNDS = 3
GROUP_HEADS = 8
EXTRA = 128


def passed_along(block, axis, distance):
    devices = range(lax.axis_size(axis))
    route = [(i - distance, i) for i in devices if i - distance in devices]
    return lax.ppermute(block, axis, route)


def shards(
    hidden, norm_gain, w_query, key_value_weight, w_out, key_value_cache, owner_slot, accepted
):
    f32, bf16 = jnp.float32, jnp.bfloat16
    rounds, rows_local, width_local = hidden.shape
    n_segment = lax.axis_size("segment")
    segment = lax.axis_index("segment")
    tensor = lax.axis_index("tensor")
    group = lax.axis_index("batch")
    requests = owner_slot.shape[0]
    rows_total = requests * DRAFT_BLOCK
    slots_local = key_value_cache.shape[1]
    kv_local = key_value_cache.shape[2]
    query_cols = w_query.shape[2]
    kv_cols = key_value_weight.shape[2]
    block = rounds * DRAFT_BLOCK
    own_rows = slots_local * block
    req_local = rows_local // DRAFT_BLOCK
    scale = HEAD_SIZE ** (-0.5)
    gain = norm_gain[0].astype(f32)
    cache_local = key_value_cache[0]

    onehot = (owner_slot[None, :] == jnp.arange(requests)[:, None]).astype(jnp.int32)
    inverse = jnp.sum(onehot * jnp.arange(requests)[None, :], axis=1)
    acc_slot = jnp.sum(onehot[None] * accepted[:, None, :], axis=2)
    acc_own = lax.dynamic_slice_in_dim(acc_slot, group * slots_local, slots_local, 1)

    rr = jnp.arange(rounds)
    jj = jnp.arange(DRAFT_BLOCK)
    sort_index = (
        rr[None, :, None] * rows_total + inverse[:, None, None] * DRAFT_BLOCK + jj[None, None, :]
    ).reshape(-1)
    own_req = tensor * req_local + jnp.arange(req_local)
    own_index = (
        owner_slot[own_req][None, :, None] * block + rr[:, None, None] * DRAFT_BLOCK + jj[None, None, :]
    ).reshape(-1)

    pos = jnp.arange(block)
    r2 = pos // DRAFT_BLOCK
    place = pos % DRAFT_BLOCK
    acc_pos = acc_own[r2, :].T
    earlier = (r2[None, None, None, :] < rr[None, :, None, None]) & (
        place[None, None, None, :] < acc_pos[:, None, None, :]
    )
    same = (r2[None, :] == rr[:, None])[:, None, :] & (place[None, None, :] <= jj[None, :, None])
    valid = earlier | same[None]
    keep = place[None, :] < acc_pos

    def layer(x_sorted):
        xf = x_sorted.astype(f32)
        sq = jnp.sum(xf * xf, axis=1, keepdims=True)
        xg = (xf * gain[None, :]).astype(bf16)
        first = jnp.dot(xg, w_query[0], preferred_element_type=f32)
        second = jnp.dot(xg, key_value_weight[0], preferred_element_type=f32)
        proj = jnp.concatenate(
            [first, second, jnp.broadcast_to(sq, (sq.shape[0], EXTRA))], axis=1
        )
        proj = lax.psum_scatter(proj, "batch", scatter_dimension=0, tiled=True)
        inv = lax.rsqrt(proj[:, query_cols + kv_cols :][:, :1] / MODEL_WIDTH + 1e-05)
        query = (proj[:, :query_cols] * inv).astype(bf16)
        keyval = (proj[:, query_cols : query_cols + kv_cols] * inv).astype(bf16)
        query_heads = query.reshape(
            slots_local, rounds, DRAFT_BLOCK, kv_local, GROUP_HEADS, HEAD_SIZE
        )
        fresh = keyval.reshape(slots_local, block, kv_local, 2 * HEAD_SIZE).transpose(0, 2, 1, 3)
        s_cache = jnp.einsum(
            "srjhgd,shld->shgrjl", query_heads, cache_local[..., :HEAD_SIZE],
            preferred_element_type=f32,
        ) * scale
        s_fresh = jnp.einsum(
            "srjhgd,shld->shgrjl", query_heads, fresh[..., :HEAD_SIZE],
            preferred_element_type=f32,
        ) * scale
        s_fresh = jnp.where(valid[:, None, None], s_fresh, -1e30)
        scores = jnp.concatenate([s_cache, s_fresh], axis=-1)
        weights = jax.nn.softmax(scores, axis=-1).astype(bf16)
        values = jnp.concatenate([cache_local[..., HEAD_SIZE:], fresh[..., HEAD_SIZE:]], axis=2)
        attended = jnp.einsum(
            "shgrjl,shld->srjhgd", weights, values, preferred_element_type=f32
        )
        attended = attended.astype(bf16).reshape(own_rows, query_cols)
        gathered = lax.all_gather(attended, "batch", axis=0, tiled=True)
        partial = jnp.dot(gathered, w_out[0], preferred_element_type=f32)
        summed = lax.psum(partial.astype(bf16), "tensor").astype(f32)
        x_new = (xf + summed).astype(bf16)
        ext_new = jnp.where(keep[:, None, :, None], fresh, jnp.zeros_like(fresh))
        return x_new, ext_new

    rows_all = lax.all_gather(hidden, "tensor", axis=1, tiled=True).reshape(-1, width_local)
    x = jnp.take(rows_all, sort_index, axis=0)
    record = None
    ext = None
    for step in range(n_segment):
        x_new, ext_new = layer(x)
        rec_new = jnp.take(x_new, own_index, axis=0).reshape(rounds, rows_local, width_local)
        if step == 0:
            record, ext = rec_new, ext_new
        else:
            active = segment == step
            record = jnp.where(active, rec_new, record)
            ext = jnp.where(active, ext_new, ext)
        if step + 1 < n_segment:
            x = passed_along(x_new, "segment", 1)
    return (record[None], ext[None])


def solution(mesh):
    in_specs = (
        P(None, "tensor", "batch"),
        P("segment", "batch"),
        P("segment", "batch", "tensor"),
        P("segment", "batch", "tensor"),
        P("segment", "tensor", "batch"),
        P("segment", "batch", "tensor", None, None),
        P(),
        P(),
    )
    out_specs = (P("segment", None, "tensor", "batch"), P("segment", "batch", "tensor", None, None))
    return jax.shard_map(shards, mesh=mesh, in_specs=in_specs, out_specs=out_specs, check_vma=False)
```

time: 947 us -> 457 us (0.48)
  blocking collectives: 712 us -> 14 us
  waiting for transfers between devices: 119 us -> 381 us
  matrix products: 44.8 us -> 17.4 us
  other arithmetic: 28.4 us -> 17.4 us
  local copies, waits for them, and re-layouts: 20.8 us -> 10.1 us
    unnamed x4 -> x0, blocking collectives: 342 us -> none
    unnamed x6 -> x8, waiting for transfers between devices: 1.28 us -> 207 us
    all_gather x12 -> x1, blocking collectives: 206 us -> 14 us  [shards(): lax.all_gather(hidden, 'tensor', axis=1, tiled=True)]
    psum x4 -> x0, blocking collectives: 164 us -> none  [shards(): total = lax.psum(jnp.sum(xf * xf, axis=1), 'batch')]
    reduce_scatter x6 -> x0, waiting for transfers between devices: 116 us -> none  [shards(): lax.psum_scatter(unsorted.astype(jnp.bfloat16), 'tensor', scatter_dimensi...]
    all_gather x0 -> x2, waiting for transfers between devices: none -> 86.2 us  [layer(): gathered = lax.all_gather(attended, 'batch', axis=0, tiled=True)]
    psum x0 -> x2, waiting for transfers between devices: none -> 85.9 us  [layer(): summed = lax.psum(partial.astype(bf16), 'tensor').astype(f32)]
    dot_general x30 -> x12, matrix products: 44.8 us -> 17.4 us  [the longest x2 10.7 us: layer(): partial = jnp.dot(gathered, w_out[0], preferred_element_type=f32)]
  transfers between devices with their start and end apart: 9 -> 7, of which waited for: 9 -> 7; matrix products, arithmetic and copies ran while one was open for 0% -> 1% of each run, Pallas kernels for 0% -> 0%
where the time goes in v1:
time: 457 us
  waiting for transfers between devices  381 us (83%)
  other arithmetic  17.4 us (4%)
  matrix products  17.4 us (4%)
  between operations  15.2 us (3%)
  blocking collectives  14 us (3%)
  local copies, waits for them, and re-layouts  10.1 us (2%)
    unnamed x8, waiting for transfers between devices  207 us
    all_gather x2, waiting for transfers between devices, layer(): gathered = lax.all_gather(attended, 'batch', axis=0, tiled=True)  86.2 us
    psum x2, waiting for transfers between devices, layer(): summed = lax.psum(partial.astype(bf16), 'tensor').astype(f32)  85.9 us
    all_gather x1, blocking collectives, shards(): lax.all_gather(hidden, 'tensor', axis=1, tiled=True)  14 us
    dot_general x2, matrix products, layer(): partial = jnp.dot(gathered, w_out[0], preferred_element_type=f32)  10.7 us
  transfers between devices with their start and end apart: 7, of which 7 were waited for; matrix products, arithmetic and copies ran while one was open for 1% of the time, Pallas kernels for 0%

profile of v1, /device:TPU:0, one launch (start us, length us, event | category | flops | bytes accessed | tf_op | source)
XLA Modules:
  0.0 456.7 jit_solution(13706285283550028622)
XLA Ops:
  9.2 14.0 %all_gather.9 = bf16[3,128,1024]{2,1,0:T(8,128)(2,1)S(1)} all-gather(bf16[3,32,1024]{2,1,0:T(8,128)(2,1)} %param.10), channel_id=1, replica_groups=mesh['segment'=2,'tensor'=4,'batch'=16] {'tensor'}, dimensions={1}, use_global_device_ids=true | all-gather | bytes 983040 | tf_op jit(solution)/shard_map/all_gather | solution.py:108
  23.2 2.1 gather_fusion
  26.3 1.2 copy-done.4
  27.5 2.0 fusion.6
  29.6 2.3 pad_maximum_fusion
  34.9 102.7 %all-reduce.11.cloned.1.call-done = f32[384,2688]{1,0:T(8,128)} async-done(((f32[384,2688]{1,0:T(8,128)}), f32[384,2688]{1,0:T(8,128)}) %all-reduce.11.cloned.1.call-update) | async-done | bytes 4128784
  137.6 0.9 fusion.60
  138.5 0.9 fusion.53
  139.5 1.0 fusion.46
  142.5 43.6 %all-gather.3.cloned.1.call-done = bf16[384,2048]{1,0:T(8,128)(2,1)} async-done(((bf16[24,2048]{1,0:T(8,128)(2,1)}), bf16[384,2048]{1,0:T(8,128)(2,1)}) %all-gather.3.cloned.1.call-update) | async-done | bytes 1572880 | tf_op jit(solution)/shard_map/all_gather | solution.py:101
  186.1 5.3 %fusion.14 = bf16[384,1024]{1,0:T(8,128)(2,1)} fusion(bf16[384,2048]{1,0:T(8,128)(2,1)} %all-gather.3.cloned.1.call-done, bf16[1,2048,1024]{2,1,0:T(8,128)(2,1)} %param.14), kind=kOutput, calls=%fused_computation.27 | convolution fusion | flops 1611005952 | bytes 6553600 | tf_op jit(solution)/shard_map/dot_general | solution.py:102
  191.5 43.7 %all-reduce.7.cloned.1.call-done = bf16[384,1024]{1,0:T(8,128)(2,1)} async-done(((bf16[384,1024]{1,0:T(8,128)(2,1)}), bf16[384,1024]{1,0:T(8,128)(2,1)}) %all-reduce.7.cloned.1.call-update) | async-done | bytes 786448 | tf_op jit(solution)/shard_map/psum | solution.py:103
  235.2 1.6 fusion.10
  236.9 1.3 collective-permute-start
  238.2 1.8 collective-permute-done
  240.9 1.8 fusion.4
  242.8 2.3 pad_maximum_fusion.1
  245.1 104.1 %all-reduce.13.cloned.1.call-done = f32[384,2688]{1,0:T(8,128)} async-done(((f32[384,2688]{1,0:T(8,128)}), f32[384,2688]{1,0:T(8,128)}) %all-reduce.13.cloned.1.call-update) | async-done | bytes 4128784
  350.1 0.9 fusion.52
  351.1 1.0 fusion.47
  355.1 42.6 %all-gather.5.cloned.1.call-done = bf16[384,2048]{1,0:T(8,128)(2,1)} async-done(((bf16[24,2048]{1,0:T(8,128)(2,1)}), bf16[384,2048]{1,0:T(8,128)(2,1)}) %all-gather.5.cloned.1.call-update) | async-done | bytes 1572880 | tf_op jit(solution)/shard_map/all_gather | solution.py:101
  397.7 5.3 %fusion.17 = bf16[384,1024]{1,0:T(8,128)(2,1)} fusion(bf16[384,2048]{1,0:T(8,128)(2,1)} %all-gather.5.cloned.1.call-done, bf16[1,2048,1024]{2,1,0:T(8,128)(2,1)} %param.14), kind=kOutput, calls=%fused_computation.28 | convolution fusion | flops 1611005952 | bytes 6553600 | tf_op jit(solution)/shard_map/dot_general | solution.py:102
  404.6 42.2 %all-reduce.9.cloned.1.call-done = bf16[384,1024]{1,0:T(8,128)(2,1)} async-done(((bf16[384,1024]{1,0:T(8,128)(2,1)}), bf16[384,1024]{1,0:T(8,128)(2,1)}) %all-reduce.9.cloned.1.call-update) | async-done | bytes 786448 | tf_op jit(solution)/shard_map/psum | solution.py:103
  446.8 1.4 fusion.13
  (98 shorter events, 15.3 us)
Async XLA Ops:
  7.2 18.5 %copy-start = (bf16[1,1024,512]{2,1,0:T(8,128)(2,1)S(1)}, bf16[1,1024,512]{2,1,0:T(8,128)(2,1)}, u32[]{:S(2)}) copy-start(bf16[1,1024,512]{2,1,0:T(8,128)(2,1)} %param.13) | copy-start | bytes 3145732
  7.2 130.5 %all-reduce.11.cloned.1.call-start = ((), (), s32[]{:S(2)}) async-start(), calls=%async_computation.4 | async-start | bytes 8257536
  25.3 2.2 copy-start.4
  31.8 0.7 copy-start.1
  31.8 0.7 copy-start.3
  31.8 1.7 copy-start.2
  31.8 1.7 copy-start.6
  31.9 154.2 %all-gather.3.cloned.1.call-start = ((), (), s32[]{:S(2)}) async-start(), calls=%async_computation | async-start | bytes 1671168 | tf_op jit(solution)/shard_map/all_gather | solution.py:101
  142.5 92.8 %all-reduce.7.cloned.1.call-start = ((), (), s32[]{:S(2)}) async-start(), calls=%async_computation.1 | async-start | bytes 1572864 | tf_op jit(solution)/shard_map/psum | solution.py:103
  191.5 157.8 %all-reduce.13.cloned.1.call-start = ((), (), s32[]{:S(2)}) async-start(), calls=%async_computation.5 | async-start | bytes 8257536
  235.2 5.6 %copy-start.5 = (bf16[1,1024,2048]{2,1,0:T(8,128)(2,1)S(1)}, bf16[1,1024,2048]{2,1,0:T(8,128)(2,1)}, u32[]{:S(2)}) copy-start(bf16[1,1024,2048]{2,1,0:T(8,128)(2,1)} %param.12) | copy-start | bytes 12582916
  236.9 3.2 collective-permute-start
  245.1 152.6 %all-gather.5.cloned.1.call-start = ((), (), s32[]{:S(2)}) async-start(), calls=%async_computation.2 | async-start | bytes 1671168 | tf_op jit(solution)/shard_map/all_gather | solution.py:101
  354.1 92.8 %all-reduce.9.cloned.1.call-start = ((), (), s32[]{:S(2)}) async-start(), calls=%async_computation.3 | async-start | bytes 1572864 | tf_op jit(solution)/shard_map/psum | solution.py:103
Sparse Core Ops, SparseCore 0:
  32.0 105.6 all-reduce.10
  142.6 43.4 all-gather.2
  191.6 43.5 all-reduce.6
  245.2 103.9 all-reduce.12
  354.2 43.4 all-gather.4
  403.2 43.5 all-reduce.8

commit v2 on v1

--- a/solution.py
+++ b/solution.py
@@ -8,7 +8,43 @@
 DRAFT_BLOCK = 4
 DECODE_ROUNDS = 3
 GROUP_HEADS = 8
-EXTRA = 128
+
+
+BATCH_INNER = 4
+
+
+def shifted(x, axis, fn):
+    n = lax.axis_size(axis)
+    return lax.ppermute(x, axis, [(i, fn(i, n)) for i in range(n)])
+
+
+def along_tensor(x, k):
+    return shifted(x, "tensor", lambda i, n: (i + k) % n)
+
+
+def along_y(x, k):
+    m = BATCH_INNER
+    return shifted(x, "batch", lambda i, n: (i // m) * m + (i % m + k) % m)
+
+
+def along_z(x, k):
+    m = BATCH_INNER
+    return shifted(x, "batch", lambda i, n: ((i // m + k) % (n // m)) * m + i % m)
+
+
+def spread(blocks, pos, send):
+    m = blocks.shape[0]
+    out = [lax.dynamic_index_in_dim(blocks, pos, 0, keepdims=False)]
+    for k in range(1, m):
+        piece = lax.dynamic_index_in_dim(blocks, (pos + k) % m, 0, keepdims=False)
+        out.append(send(piece, k))
+    return out
+
+
+def gather_from(x, pos, m, send):
+    out = [x] + [send(x, k) for k in range(1, m)]
+    order = (pos - jnp.arange(m)) % m
+    return jnp.take(jnp.stack(out), order, axis=0)
 
 
 def passed_along(block, axis, distance):
@@ -65,19 +101,29 @@
     valid = earlier | same[None]
     keep = place[None, :] < acc_pos
 
+    n_tensor = lax.axis_size("tensor")
+    n_y = BATCH_INNER
+    n_z = lax.axis_size("batch") // n_y
+    z_pos = group // n_y
+    y_pos = group % n_y
+
     def layer(x_sorted):
         xf = x_sorted.astype(f32)
-        sq = jnp.sum(xf * xf, axis=1, keepdims=True)
+        sq = jnp.sum(xf * xf, axis=1)
         xg = (xf * gain[None, :]).astype(bf16)
         first = jnp.dot(xg, w_query[0], preferred_element_type=f32)
         second = jnp.dot(xg, key_value_weight[0], preferred_element_type=f32)
-        proj = jnp.concatenate(
-            [first, second, jnp.broadcast_to(sq, (sq.shape[0], EXTRA))], axis=1
-        )
-        proj = lax.psum_scatter(proj, "batch", scatter_dimension=0, tiled=True)
-        inv = lax.rsqrt(proj[:, query_cols + kv_cols :][:, :1] / MODEL_WIDTH + 1e-05)
-        query = (proj[:, :query_cols] * inv).astype(bf16)
-        keyval = (proj[:, query_cols : query_cols + kv_cols] * inv).astype(bf16)
+        proj = jnp.concatenate([first, second], axis=1)
+        cols = proj.shape[1]
+        by_y = proj.astype(bf16).reshape(n_z, n_y, own_rows, cols).transpose(1, 0, 2, 3)
+        sq_y = sq.reshape(n_z, n_y, own_rows).transpose(1, 0, 2)
+        part = sum(r.astype(f32) for r in spread(by_y, y_pos, along_y))
+        part_sq = sum(spread(sq_y, y_pos, along_y))
+        total = sum(spread(part, z_pos, along_z))
+        total_sq = sum(spread(part_sq, z_pos, along_z))
+        inv = lax.rsqrt(total_sq / MODEL_WIDTH + 1e-05)[:, None]
+        query = (total[:, :query_cols] * inv).astype(bf16)
+        keyval = (total[:, query_cols:] * inv).astype(bf16)
         query_heads = query.reshape(
             slots_local, rounds, DRAFT_BLOCK, kv_local, GROUP_HEADS, HEAD_SIZE
         )
@@ -98,14 +144,23 @@
             "shgrjl,shld->srjhgd", weights, values, preferred_element_type=f32
         )
         attended = attended.astype(bf16).reshape(own_rows, query_cols)
-        gathered = lax.all_gather(attended, "batch", axis=0, tiled=True)
+        by_z = gather_from(attended, z_pos, n_z, along_z)
+        by_zy = gather_from(by_z, y_pos, n_y, along_y)
+        gathered = by_zy.transpose(1, 0, 2, 3).reshape(-1, query_cols)
         partial = jnp.dot(gathered, w_out[0], preferred_element_type=f32)
-        summed = lax.psum(partial.astype(bf16), "tensor").astype(f32)
-        x_new = (xf + summed).astype(bf16)
+        quarter = partial.shape[0] // n_tensor
+        pieces = partial.astype(bf16).reshape(n_tensor, quarter, width_local)
+        mine = sum(r.astype(f32) for r in spread(pieces, tensor, along_tensor))
+        x_mine = lax.dynamic_index_in_dim(
+            xf.reshape(n_tensor, quarter, width_local), tensor, 0, keepdims=False
+        )
+        x_mine = (x_mine + mine).astype(bf16)
+        x_new = gather_from(x_mine, tensor, n_tensor, along_tensor).reshape(-1, width_local)
         ext_new = jnp.where(keep[:, None, :, None], fresh, jnp.zeros_like(fresh))
         return x_new, ext_new
 
-    rows_all = lax.all_gather(hidden, "tensor", axis=1, tiled=True).reshape(-1, width_local)
+    rows_all = gather_from(hidden, tensor, n_tensor, along_tensor)
+    rows_all = rows_all.transpose(1, 0, 2, 3).reshape(-1, width_local)
     x = jnp.take(rows_all, sort_index, axis=0)
     record = None
     ext = None

time: 457 us -> 257 us (0.56)
  waiting for transfers between devices: 381 us -> 123 us
  starting transfers between devices: 1.59 us -> 76.2 us
  blocking collectives: 14 us -> 0 us
  between operations: 15.2 us -> 1.54 us
  local copies, waits for them, and re-layouts: 10.1 us -> 19.1 us
    unnamed x8 -> x0, waiting for transfers between devices: 207 us -> none
    ppermute x0 -> x51, waiting for transfers between devices: none -> 122 us  [shifted(): return lax.ppermute(x, axis, [(i, fn(i, n)) for i in range(n)])]
    all_gather x2 -> x0, waiting for transfers between devices: 86.2 us -> none  [layer(): gathered = lax.all_gather(attended, 'batch', axis=0, tiled=True)]
    psum x2 -> x0, waiting for transfers between devices: 85.9 us -> none  [layer(): summed = lax.psum(partial.astype(bf16), 'tensor').astype(f32)]
    ppermute x0 -> x51, starting transfers between devices: none -> 74.8 us  [shifted(): return lax.ppermute(x, axis, [(i, fn(i, n)) for i in range(n)])]
    all_gather x1 -> x0, blocking collectives: 14 us -> none  [shards(): lax.all_gather(hidden, 'tensor', axis=1, tiled=True)]
    dot_general x2, matrix products: 10.7 us -> 3.63 us  [layer(): partial = jnp.dot(gathered, w_out[0], preferred_element_type=f32)]
    gather x0 -> x7, local copies, waits for them, and re-layouts: none -> 6.57 us  [gather_from(): return jnp.take(jnp.stack(out), order, axis=0)]
  transfers between devices with their start and end apart: 7 -> 52, of which waited for: 7 -> 32; matrix products, arithmetic and copies ran while one was open for 1% -> 4% of each run, Pallas kernels for 0% -> 0%
where the time goes in v2:
time: 257 us; the launch traced here: 256 us
  waiting for transfers between devices  123 us (48%)
  starting transfers between devices  76.2 us (30%)
  other arithmetic  20.3 us (8%)
  local copies, waits for them, and re-layouts  19.1 us (7%)
  matrix products  15.7 us (6%)
    ppermute x51, waiting for transfers between devices, shifted(): return lax.ppermute(x, axis, [(i, fn(i, n)) for i in range(n)])  122 us
    ppermute x51, starting transfers between devices, shifted(): return lax.ppermute(x, axis, [(i, fn(i, n)) for i in range(n)])  74.8 us
    dot_general x2, matrix products, layer(): first = jnp.dot(xg, w_query[0], preferred_element_type=f32)  8.24 us
    gather x7, local copies, waits for them, and re-layouts, gather_from(): return jnp.take(jnp.stack(out), order, axis=0)  6.57 us
  transfers between devices with their start and end apart: 52, of which 32 were waited for; matrix products, arithmetic and copies ran while one was open for 4% of the time, Pallas kernels for 0%

profile of v2, /device:TPU:0, one launch (start us, length us, event | category | flops | bytes accessed | tf_op | source)
XLA Modules:
  0.0 256.1 jit_solution(6980416803210043357)
XLA Ops:
  10.6 3.5 %collective-permute-done.1 = bf16[3,32,1024]{2,1,0:T(8,128)(2,1)S(1)} collective-permute-done((bf16[3,32,1024]{2,1,0:T(8,128)(2,1)}, bf16[3,32,1024]{2,1,0:T(8,128)(2,1)S(1)}, u32[]{:S(2)}, u32[]{:S(2)}) %collective-permute-start.1) | collective-permute-done | bytes 196640 | tf_op jit(solution)/shard_map/ppermute | solution.py:18
  18.8 4.3 %fusion.8 = bf16[4,4,24,2048]{3,2,1,0:T(8,128)(2,1)S(1)} fusion(bf16[1,1024,2048]{2,1,0:T(8,128)(2,1)} %param.18, f32[1024]{0:T(1024)S(1)} %bitcast.335, bf16[4,4,24,1,1024]{4,2,1,0,3:T(8,128)(2,1)S(1)} %bitcast.287, pred[4,4,24]{2,1,0:T(4,128)(4,1)S(1)} %broadcast_in_dim.137), kind=kOutput, calls=%fused_computation.28 | convolution fusion | flops 1612972032 | bytes 6558080 | tf_op jit(solution)/shard_map/dot_general | solution.py:114
  34.3 14.8 %collective-permute-done.11 = f32[4,24]{1,0:T(4,128)S(1)} collective-permute-done((f32[4,24]{1,0:T(4,128)S(1)}, f32[4,24]{1,0:T(4,128)S(1)}, u32[]{:S(2)}, u32[]{:S(2)}) %collective-permute-start.11) | collective-permute-done | bytes 416 | tf_op jit(solution)/shard_map/ppermute | solution.py:18
  49.1 3.1 %collective-permute-start.10 = (f32[4,24]{1,0:T(4,128)S(1)}, f32[4,24]{1,0:T(4,128)S(1)}, u32[]{:S(2)}, u32[]{:S(2)}) collective-permute-start(f32[4,24]{1,0:T(4,128)S(1)} %bitcast.339), channel_id=1, source_target_pairs={{0,2},{1,3},{2,0},{3,1},{4,6},{5,7},{6,4},{7,5},{8,10},{9,11},{10,... | collective-permute-start | bytes 1160 | tf_op jit(solution)/shard_map/ppermute | solution.py:18
  66.9 4.4 %collective-permute-start.13 = (f32[24]{0:T(128)S(1)}, f32[24]{0:T(128)S(1)}, u32[]{:S(2)}, u32[]{:S(2)}) collective-permute-start(f32[24]{0:T(128)S(1)} %get-tuple-element.45), channel_id=1, source_target_pairs={{0,8},{1,9},{2,10},{3,11},{4,12},{5,13},{6,14},{7,15},{8,0},{9,1},... | collective-permute-start | bytes 296 | tf_op jit(solution)/shard_map/ppermute | solution.py:18
  74.4 3.2 %collective-permute-start.17 = (bf16[24,2048]{1,0:T(8,128)(2,1)S(1)}, bf16[24,2048]{1,0:T(8,128)(2,1)S(1)}, u32[]{:S(2)}, u32[]{:S(2)}) collective-permute-start(bf16[24,2048]{1,0:T(8,128)(2,1)S(1)} %reshape.619), channel_id=1, source_target_pairs={{0,12},{1,13},{2,14},{3,15},{4,0},{5,1},{6,2},{7,3},{8,4},{9,5},{1... | collective-permute-start | bytes 294920 | tf_op jit(solution)/shard_map/ppermute | solution.py:18
  79.9 4.0 %collective-permute-done.16 = bf16[24,2048]{1,0:T(8,128)(2,1)S(1)} collective-permute-done((bf16[24,2048]{1,0:T(8,128)(2,1)S(1)}, bf16[24,2048]{1,0:T(8,128)(2,1)S(1)}, u32[]{:S(2)}, u32[]{:S(2)}) %collective-permute-start.16) | collective-permute-done | bytes 98336 | tf_op jit(solution)/shard_map/ppermute | solution.py:18
  91.1 5.8 %collective-permute-done.19 = bf16[4,24,2048]{2,1,0:T(8,128)(2,1)S(1)} collective-permute-done((bf16[4,24,2048]{2,1,0:T(8,128)(2,1)S(1)}, bf16[4,24,2048]{2,1,0:T(8,128)(2,1)S(1)}, u32[]{:S(2)}, u32[]{:S(2)}) %collective-permute-start.19) | collective-permute-done | bytes 393248 | tf_op jit(solution)/shard_map/ppermute | solution.py:18
  96.9 4.1 %collective-permute-done.18 = bf16[4,24,2048]{2,1,0:T(8,128)(2,1)S(1)} collective-permute-done((bf16[4,24,2048]{2,1,0:T(8,128)(2,1)S(1)}, bf16[4,24,2048]{2,1,0:T(8,128)(2,1)S(1)}, u32[]{:S(2)}, u32[]{:S(2)}) %collective-permute-start.18) | collective-permute-done | bytes 393248 | tf_op jit(solution)/shard_map/ppermute | solution.py:18
  112.8 4.8 %collective-permute-done.21 = bf16[96,1024]{1,0:T(8,128)(2,1)S(1)} collective-permute-done((bf16[96,1024]{1,0:T(8,128)(2,1)S(1)}, bf16[96,1024]{1,0:T(8,128)(2,1)S(1)}, u32[]{:S(2)}, u32[]{:S(2)}) %collective-permute-start.21) | collective-permute-done | bytes 196640 | tf_op jit(solution)/shard_map/ppermute | solution.py:18
  123.5 4.4 %collective-permute-done.26 = bf16[96,1024]{1,0:T(8,128)(2,1)S(1)} collective-permute-done((bf16[96,1024]{1,0:T(8,128)(2,1)S(1)}, bf16[96,1024]{1,0:T(8,128)(2,1)S(1)}, u32[]{:S(2)}, u32[]{:S(2)}) %collective-permute-start.26) | collective-permute-done | bytes 196640 | tf_op jit(solution)/shard_map/ppermute | solution.py:18
  137.9 4.0 %fusion.11 = bf16[4,4,24,2048]{3,2,1,0:T(8,128)(2,1)S(1)} fusion(bf16[4,4,24,1024]{3,2,1,0:T(8,128)(2,1)S(1)} %bitcast.303, bf16[1,1024,2048]{2,1,0:T(8,128)(2,1)} %param.18), kind=kOutput, calls=%fused_computation.29 | convolution fusion | flops 1611399168 | bytes 6553600 | tf_op jit(solution)/shard_map/dot_general | solution.py:114
  144.7 4.2 %collective-permute-start.29 = (bf16[4,24,2560]{2,1,0:T(8,128)(2,1)}, bf16[4,24,2560]{2,1,0:T(8,128)(2,1)}, u32[]{:S(2)}, u32[]{:S(2)}) collective-permute-start(bf16[4,24,2560]{2,1,0:T(8,128)(2,1)} %get-tuple-element.13), channel_id=1, source_target_pairs={{0,2},{1,3},{2,0},{3,1},{4,6},{5,7},{6,4},{7,5},{8,10},{9,11},{10,... | collective-permute-start | bytes 1474568 | tf_op jit(solution)/shard_map/ppermute | solution.py:18
  151.1 19.6 %collective-permute-done.36 = f32[4,24]{1,0:T(4,128)S(1)} collective-permute-done((f32[4,24]{1,0:T(4,128)S(1)}, f32[4,24]{1,0:T(4,128)S(1)}, u32[]{:S(2)}, u32[]{:S(2)}) %collective-permute-start.36) | collective-permute-done | bytes 416 | tf_op jit(solution)/shard_map/ppermute | solution.py:18
  171.7 4.1 %collective-permute-done.35 = f32[4,24]{1,0:T(4,128)S(1)} collective-permute-done((f32[4,24]{1,0:T(4,128)S(1)}, f32[4,24]{1,0:T(4,128)S(1)}, u32[]{:S(2)}, u32[]{:S(2)}) %collective-permute-start.35) | collective-permute-done | bytes 416 | tf_op jit(solution)/shard_map/ppermute | solution.py:18
  177.5 3.2 %collective-permute-start.33 = (f32[24,2560]{1,0:T(8,128)S(1)}, f32[24,2560]{1,0:T(8,128)S(1)}, u32[]{:S(2)}, u32[]{:S(2)}) collective-permute-start(f32[24,2560]{1,0:T(8,128)S(1)} %get-tuple-element.19), channel_id=1, source_target_pairs={{0,12},{1,13},{2,14},{3,15},{4,0},{5,1},{6,2},{7,3},{8,4},{9,5},{1... | collective-permute-start | bytes 737288 | tf_op jit(solution)/shard_map/ppermute | solution.py:18
  184.5 5.8 %collective-permute-done.37 = f32[24]{0:T(128)S(1)} collective-permute-done((f32[24]{0:T(128)S(1)}, f32[24]{0:T(128)S(1)}, u32[]{:S(2)}, u32[]{:S(2)}) %collective-permute-start.37) | collective-permute-done | bytes 128 | tf_op jit(solution)/shard_map/ppermute | solution.py:18
  190.3 5.1 %collective-permute-done.38 = f32[24]{0:T(128)S(1)} collective-permute-done((f32[24]{0:T(128)S(1)}, f32[24]{0:T(128)S(1)}, u32[]{:S(2)}, u32[]{:S(2)}) %collective-permute-start.38) | collective-permute-done | bytes 128 | tf_op jit(solution)/shard_map/ppermute | solution.py:18
  206.2 3.0 %collective-permute-start.43 = (bf16[4,24,2048]{2,1,0:T(8,128)(2,1)S(1)}, bf16[4,24,2048]{2,1,0:T(8,128)(2,1)S(1)}, u32[]{:S(2)}, u32[]{:S(2)}) collective-permute-start(bf16[4,24,2048]{2,1,0:T(8,128)(2,1)S(1)} %broadcast_select_fusion.2), channel_id=1, source_target_pairs={{0,1},{1,2},{2,3},{3,0},{4,5},{5,6},{6,7},{7,4},{8,9},{9,10},{10,1... | collective-permute-start | bytes 1179656 | tf_op jit(solution)/shard_map/ppermute | solution.py:18
  209.5 8.1 %collective-permute-done.44 = bf16[4,24,2048]{2,1,0:T(8,128)(2,1)S(1)} collective-permute-done((bf16[4,24,2048]{2,1,0:T(8,128)(2,1)S(1)}, bf16[4,24,2048]{2,1,0:T(8,128)(2,1)S(1)}, u32[]{:S(2)}, u32[]{:S(2)}) %collective-permute-start.44) | collective-permute-done | bytes 393248 | tf_op jit(solution)/shard_map/ppermute | solution.py:18
  217.6 4.2 %collective-permute-done.43 = bf16[4,24,2048]{2,1,0:T(8,128)(2,1)S(1)} collective-permute-done((bf16[4,24,2048]{2,1,0:T(8,128)(2,1)S(1)}, bf16[4,24,2048]{2,1,0:T(8,128)(2,1)S(1)}, u32[]{:S(2)}, u32[]{:S(2)}) %collective-permute-start.43) | collective-permute-done | bytes 393248 | tf_op jit(solution)/shard_map/ppermute | solution.py:18
  229.7 3.2 %collective-permute-start.48 = (bf16[96,1024]{1,0:T(8,128)(2,1)}, bf16[96,1024]{1,0:T(8,128)(2,1)}, u32[]{:S(2)}, u32[]{:S(2)}) collective-permute-start(bf16[96,1024]{1,0:T(8,128)(2,1)} %get-tuple-element.25), channel_id=1, source_target_pairs={{0,48},{16,0},{32,16},{48,32},{1,49},{17,1},{33,17},{49,33},{2,50}... | collective-permute-start | bytes 589832 | tf_op jit(solution)/shard_map/ppermute | solution.py:18
  234.6 6.5 %collective-permute-done.46 = bf16[96,1024]{1,0:T(8,128)(2,1)} collective-permute-done((bf16[96,1024]{1,0:T(8,128)(2,1)}, bf16[96,1024]{1,0:T(8,128)(2,1)}, u32[]{:S(2)}, u32[]{:S(2)}) %collective-permute-start.46) | collective-permute-done | bytes 196640 | tf_op jit(solution)/shard_map/ppermute | solution.py:18
  246.3 3.7 %collective-permute-done.51 = bf16[96,1024]{1,0:T(8,128)(2,1)S(1)} collective-permute-done((bf16[96,1024]{1,0:T(8,128)(2,1)S(1)}, bf16[96,1024]{1,0:T(8,128)(2,1)S(1)}, u32[]{:S(2)}, u32[]{:S(2)}) %collective-permute-start.51) | collective-permute-done | bytes 196640 | tf_op jit(solution)/shard_map/ppermute | solution.py:18
  (246 shorter events, 123.7 us)
Async XLA Ops:
  24.2 30.0 %collective-permute-start.3 = (bf16[4,24,2560]{2,1,0:T(8,128)(2,1)}, bf16[4,24,2560]{2,1,0:T(8,128)(2,1)}, u32[]{:S(2)}, u32[]{:S(2)}) collective-permute-start(bf16[4,24,2560]{2,1,0:T(8,128)(2,1)} %get-tuple-element.15), channel_id=1, source_target_pairs={{0,1},{1,2},{2,3},{3,0},{4,5},{5,6},{6,7},{7,4},{8,9},{9,10},{10,1... | collective-permute-start | bytes 1474568 | tf_op jit(solution)/shard_map/ppermute | solution.py:18
  25.8 28.4 %collective-permute-start.4 = (bf16[4,24,2560]{2,1,0:T(8,128)(2,1)}, bf16[4,24,2560]{2,1,0:T(8,128)(2,1)}, u32[]{:S(2)}, u32[]{:S(2)}) collective-permute-start(bf16[4,24,2560]{2,1,0:T(8,128)(2,1)} %get-tuple-element.16), channel_id=1, source_target_pairs={{0,2},{1,3},{2,0},{3,1},{4,6},{5,7},{6,4},{7,5},{8,10},{9,11},{10,... | collective-permute-start | bytes 1474568 | tf_op jit(solution)/shard_map/ppermute | solution.py:18
  28.7 25.5 %collective-permute-start.5 = (bf16[4,24,2560]{2,1,0:T(8,128)(2,1)}, bf16[4,24,2560]{2,1,0:T(8,128)(2,1)}, u32[]{:S(2)}, u32[]{:S(2)}) collective-permute-start(bf16[4,24,2560]{2,1,0:T(8,128)(2,1)} %get-tuple-element.17), channel_id=1, source_target_pairs={{0,3},{1,0},{2,1},{3,2},{4,7},{5,4},{6,5},{7,6},{8,11},{9,8},{10,9... | collective-permute-start | bytes 1474568 | tf_op jit(solution)/shard_map/ppermute | solution.py:18
  30.5 18.6 %collective-permute-start.11 = (f32[4,24]{1,0:T(4,128)S(1)}, f32[4,24]{1,0:T(4,128)S(1)}, u32[]{:S(2)}, u32[]{:S(2)}) collective-permute-start(f32[4,24]{1,0:T(4,128)S(1)} %bitcast.343), channel_id=1, source_target_pairs={{0,3},{1,0},{2,1},{3,2},{4,7},{5,4},{6,5},{7,6},{8,11},{9,8},{10,9... | collective-permute-start | bytes 1160 | tf_op jit(solution)/shard_map/ppermute | solution.py:18
  32.3 19.9 %collective-permute-start.9 = (f32[4,24]{1,0:T(4,128)S(1)}, f32[4,24]{1,0:T(4,128)S(1)}, u32[]{:S(2)}, u32[]{:S(2)}) collective-permute-start(f32[4,24]{1,0:T(4,128)S(1)} %bitcast.340), channel_id=1, source_target_pairs={{0,1},{1,2},{2,3},{3,0},{4,5},{5,6},{6,7},{7,4},{8,9},{9,10},{10,1... | collective-permute-start | bytes 1160 | tf_op jit(solution)/shard_map/ppermute | solution.py:18
  55.9 17.0 %collective-permute-start.6 = (f32[24,2560]{1,0:T(8,128)S(1)}, f32[24,2560]{1,0:T(8,128)S(1)}, u32[]{:S(2)}, u32[]{:S(2)}) collective-permute-start(f32[24,2560]{1,0:T(8,128)S(1)} %get-tuple-element.21), channel_id=1, source_target_pairs={{0,4},{1,5},{2,6},{3,7},{4,8},{5,9},{6,10},{7,11},{8,12},{9,13},{1... | collective-permute-start | bytes 737288 | tf_op jit(solution)/shard_map/ppermute | solution.py:18
  57.8 15.0 %collective-permute-start.8 = (f32[24,2560]{1,0:T(8,128)S(1)}, f32[24,2560]{1,0:T(8,128)S(1)}, u32[]{:S(2)}, u32[]{:S(2)}) collective-permute-start(f32[24,2560]{1,0:T(8,128)S(1)} %get-tuple-element.22), channel_id=1, source_target_pairs={{0,12},{1,13},{2,14},{3,15},{4,0},{5,1},{6,2},{7,3},{8,4},{9,5},{1... | collective-permute-start | bytes 737288 | tf_op jit(solution)/shard_map/ppermute | solution.py:18
  60.0 12.8 %collective-permute-start.7 = (f32[24,2560]{1,0:T(8,128)S(1)}, f32[24,2560]{1,0:T(8,128)S(1)}, u32[]{:S(2)}, u32[]{:S(2)}) collective-permute-start(f32[24,2560]{1,0:T(8,128)S(1)} %get-tuple-element.23), channel_id=1, source_target_pairs={{0,8},{1,9},{2,10},{3,11},{4,12},{5,13},{6,14},{7,15},{8,0},{9,1},... | collective-permute-start | bytes 737288 | tf_op jit(solution)/shard_map/ppermute | solution.py:18
  85.6 11.3 %collective-permute-start.19 = (bf16[4,24,2048]{2,1,0:T(8,128)(2,1)S(1)}, bf16[4,24,2048]{2,1,0:T(8,128)(2,1)S(1)}, u32[]{:S(2)}, u32[]{:S(2)}) collective-permute-start(bf16[4,24,2048]{2,1,0:T(8,128)(2,1)S(1)} %broadcast_select_fusion.3), channel_id=1, source_target_pairs={{0,2},{1,3},{2,0},{3,1},{4,6},{5,7},{6,4},{7,5},{8,10},{9,11},{10,... | collective-permute-start | bytes 1179656 | tf_op jit(solution)/shard_map/ppermute | solution.py:18
  87.8 13.2 %collective-permute-start.18 = (bf16[4,24,2048]{2,1,0:T(8,128)(2,1)S(1)}, bf16[4,24,2048]{2,1,0:T(8,128)(2,1)S(1)}, u32[]{:S(2)}, u32[]{:S(2)}) collective-permute-start(bf16[4,24,2048]{2,1,0:T(8,128)(2,1)S(1)} %broadcast_select_fusion.3), channel_id=1, source_target_pairs={{0,1},{1,2},{2,3},{3,0},{4,5},{5,6},{6,7},{7,4},{8,9},{9,10},{10,1... | collective-permute-start | bytes 1179656 | tf_op jit(solution)/shard_map/ppermute | solution.py:18
  90.0 12.9 %collective-permute-start.20 = (bf16[4,24,2048]{2,1,0:T(8,128)(2,1)S(1)}, bf16[4,24,2048]{2,1,0:T(8,128)(2,1)S(1)}, u32[]{:S(2)}, u32[]{:S(2)}) collective-permute-start(bf16[4,24,2048]{2,1,0:T(8,128)(2,1)S(1)} %broadcast_select_fusion.3), channel_id=1, source_target_pairs={{0,3},{1,0},{2,1},{3,2},{4,7},{5,4},{6,5},{7,6},{8,11},{9,8},{10,9... | collective-permute-start | bytes 1179656 | tf_op jit(solution)/shard_map/ppermute | solution.py:18
  144.2 31.6 %collective-permute-start.28 = (bf16[4,24,2560]{2,1,0:T(8,128)(2,1)}, bf16[4,24,2560]{2,1,0:T(8,128)(2,1)}, u32[]{:S(2)}, u32[]{:S(2)}) collective-permute-start(bf16[4,24,2560]{2,1,0:T(8,128)(2,1)} %get-tuple-element.12), channel_id=1, source_target_pairs={{0,1},{1,2},{2,3},{3,0},{4,5},{5,6},{6,7},{7,4},{8,9},{9,10},{10,1... | collective-permute-start | bytes 1474568 | tf_op jit(solution)/shard_map/ppermute | solution.py:18
  144.7 31.1 %collective-permute-start.29 = (bf16[4,24,2560]{2,1,0:T(8,128)(2,1)}, bf16[4,24,2560]{2,1,0:T(8,128)(2,1)}, u32[]{:S(2)}, u32[]{:S(2)}) collective-permute-start(bf16[4,24,2560]{2,1,0:T(8,128)(2,1)} %get-tuple-element.13), channel_id=1, source_target_pairs={{0,2},{1,3},{2,0},{3,1},{4,6},{5,7},{6,4},{7,5},{8,10},{9,11},{10,... | collective-permute-start | bytes 1474568 | tf_op jit(solution)/shard_map/ppermute | solution.py:18
  148.9 26.9 %collective-permute-start.30 = (bf16[4,24,2560]{2,1,0:T(8,128)(2,1)}, bf16[4,24,2560]{2,1,0:T(8,128)(2,1)}, u32[]{:S(2)}, u32[]{:S(2)}) collective-permute-start(bf16[4,24,2560]{2,1,0:T(8,128)(2,1)} %get-tuple-element.14), channel_id=1, source_target_pairs={{0,3},{1,0},{2,1},{3,2},{4,7},{5,4},{6,5},{7,6},{8,11},{9,8},{10,9... | collective-permute-start | bytes 1474568 | tf_op jit(solution)/shard_map/ppermute | solution.py:18
  148.9 21.8 %collective-permute-start.36 = (f32[4,24]{1,0:T(4,128)S(1)}, f32[4,24]{1,0:T(4,128)S(1)}, u32[]{:S(2)}, u32[]{:S(2)}) collective-permute-start(f32[4,24]{1,0:T(4,128)S(1)} %bitcast.344), channel_id=1, source_target_pairs={{0,3},{1,0},{2,1},{3,2},{4,7},{5,4},{6,5},{7,6},{8,11},{9,8},{10,9... | collective-permute-start | bytes 1160 | tf_op jit(solution)/shard_map/ppermute | solution.py:18
  149.5 22.2 %collective-permute-start.34 = (f32[4,24]{1,0:T(4,128)S(1)}, f32[4,24]{1,0:T(4,128)S(1)}, u32[]{:S(2)}, u32[]{:S(2)}) collective-permute-start(f32[4,24]{1,0:T(4,128)S(1)} %bitcast.342), channel_id=1, source_target_pairs={{0,1},{1,2},{2,3},{3,0},{4,5},{5,6},{6,7},{7,4},{8,9},{9,10},{10,1... | collective-permute-start | bytes 1160 | tf_op jit(solution)/shard_map/ppermute | solution.py:18
  177.4 18.0 %collective-permute-start.31 = (f32[24,2560]{1,0:T(8,128)S(1)}, f32[24,2560]{1,0:T(8,128)S(1)}, u32[]{:S(2)}, u32[]{:S(2)}) collective-permute-start(f32[24,2560]{1,0:T(8,128)S(1)} %get-tuple-element.18), channel_id=1, source_target_pairs={{0,4},{1,5},{2,6},{3,7},{4,8},{5,9},{6,10},{7,11},{8,12},{9,13},{1... | collective-permute-start | bytes 737288 | tf_op jit(solution)/shard_map/ppermute | solution.py:18
  177.5 17.9 %collective-permute-start.33 = (f32[24,2560]{1,0:T(8,128)S(1)}, f32[24,2560]{1,0:T(8,128)S(1)}, u32[]{:S(2)}, u32[]{:S(2)}) collective-permute-start(f32[24,2560]{1,0:T(8,128)S(1)} %get-tuple-element.19), channel_id=1, source_target_pairs={{0,12},{1,13},{2,14},{3,15},{4,0},{5,1},{6,2},{7,3},{8,4},{9,5},{1... | collective-permute-start | bytes 737288 | tf_op jit(solution)/shard_map/ppermute | solution.py:18
  180.7 14.7 %collective-permute-start.32 = (f32[24,2560]{1,0:T(8,128)S(1)}, f32[24,2560]{1,0:T(8,128)S(1)}, u32[]{:S(2)}, u32[]{:S(2)}) collective-permute-start(f32[24,2560]{1,0:T(8,128)S(1)} %get-tuple-element.20), channel_id=1, source_target_pairs={{0,8},{1,9},{2,10},{3,11},{4,12},{5,13},{6,14},{7,15},{8,0},{9,1},... | collective-permute-start | bytes 737288 | tf_op jit(solution)/shard_map/ppermute | solution.py:18
  205.1 12.5 %collective-permute-start.44 = (bf16[4,24,2048]{2,1,0:T(8,128)(2,1)S(1)}, bf16[4,24,2048]{2,1,0:T(8,128)(2,1)S(1)}, u32[]{:S(2)}, u32[]{:S(2)}) collective-permute-start(bf16[4,24,2048]{2,1,0:T(8,128)(2,1)S(1)} %broadcast_select_fusion.2), channel_id=1, source_target_pairs={{0,2},{1,3},{2,0},{3,1},{4,6},{5,7},{6,4},{7,5},{8,10},{9,11},{10,... | collective-permute-start | bytes 1179656 | tf_op jit(solution)/shard_map/ppermute | solution.py:18
  206.2 15.6 %collective-permute-start.43 = (bf16[4,24,2048]{2,1,0:T(8,128)(2,1)S(1)}, bf16[4,24,2048]{2,1,0:T(8,128)(2,1)S(1)}, u32[]{:S(2)}, u32[]{:S(2)}) collective-permute-start(bf16[4,24,2048]{2,1,0:T(8,128)(2,1)S(1)} %broadcast_select_fusion.2), channel_id=1, source_target_pairs={{0,1},{1,2},{2,3},{3,0},{4,5},{5,6},{6,7},{7,4},{8,9},{9,10},{10,1... | collective-permute-start | bytes 1179656 | tf_op jit(solution)/shard_map/ppermute | solution.py:18
  209.2 13.1 %collective-permute-start.45 = (bf16[4,24,2048]{2,1,0:T(8,128)(2,1)S(1)}, bf16[4,24,2048]{2,1,0:T(8,128)(2,1)S(1)}, u32[]{:S(2)}, u32[]{:S(2)}) collective-permute-start(bf16[4,24,2048]{2,1,0:T(8,128)(2,1)S(1)} %broadcast_select_fusion.2), channel_id=1, source_target_pairs={{0,3},{1,0},{2,1},{3,2},{4,7},{5,4},{6,5},{7,6},{8,11},{9,8},{10,9... | collective-permute-start | bytes 1179656 | tf_op jit(solution)/shard_map/ppermute | solution.py:18
  229.7 11.4 %collective-permute-start.46 = (bf16[96,1024]{1,0:T(8,128)(2,1)}, bf16[96,1024]{1,0:T(8,128)(2,1)}, u32[]{:S(2)}, u32[]{:S(2)}) collective-permute-start(bf16[96,1024]{1,0:T(8,128)(2,1)} %get-tuple-element.24), channel_id=1, source_target_pairs={{0,16},{16,32},{32,48},{48,0},{1,17},{17,33},{33,49},{49,1},{2,18}... | collective-permute-start | bytes 589832 | tf_op jit(solution)/shard_map/ppermute | solution.py:18
  229.7 11.4 %collective-permute-start.48 = (bf16[96,1024]{1,0:T(8,128)(2,1)}, bf16[96,1024]{1,0:T(8,128)(2,1)}, u32[]{:S(2)}, u32[]{:S(2)}) collective-permute-start(bf16[96,1024]{1,0:T(8,128)(2,1)} %get-tuple-element.25), channel_id=1, source_target_pairs={{0,48},{16,0},{32,16},{48,32},{1,49},{17,1},{33,17},{49,33},{2,50}... | collective-permute-start | bytes 589832 | tf_op jit(solution)/shard_map/ppermute | solution.py:18
  (40 other events, 273.5 us)

commit v3 on v2

--- a/solution.py
+++ b/solution.py
@@ -107,23 +107,27 @@
     z_pos = group // n_y
     y_pos = group % n_y
 
-    def layer(x_sorted):
+    back_index = (
+        owner_slot[None, :, None] * block + rr[:, None, None] * DRAFT_BLOCK + jj[None, None, :]
+    ).reshape(-1)
+
+    def layer(x_sorted, last):
         xf = x_sorted.astype(f32)
-        sq = jnp.sum(xf * xf, axis=1)
+        sq = jnp.sum(xf * xf, axis=1, keepdims=True)
+        sq_hi = sq.astype(bf16)
+        sq_lo = (sq - sq_hi.astype(f32)).astype(bf16)
         xg = (xf * gain[None, :]).astype(bf16)
         first = jnp.dot(xg, w_query[0], preferred_element_type=f32)
         second = jnp.dot(xg, key_value_weight[0], preferred_element_type=f32)
-        proj = jnp.concatenate([first, second], axis=1)
+        proj = jnp.concatenate([first.astype(bf16), second.astype(bf16), sq_hi, sq_lo], axis=1)
         cols = proj.shape[1]
-        by_y = proj.astype(bf16).reshape(n_z, n_y, own_rows, cols).transpose(1, 0, 2, 3)
-        sq_y = sq.reshape(n_z, n_y, own_rows).transpose(1, 0, 2)
+        by_y = proj.reshape(n_z, n_y, own_rows, cols).transpose(1, 0, 2, 3)
         part = sum(r.astype(f32) for r in spread(by_y, y_pos, along_y))
-        part_sq = sum(spread(sq_y, y_pos, along_y))
         total = sum(spread(part, z_pos, along_z))
-        total_sq = sum(spread(part_sq, z_pos, along_z))
+        total_sq = total[:, query_cols + kv_cols] + total[:, query_cols + kv_cols + 1]
         inv = lax.rsqrt(total_sq / MODEL_WIDTH + 1e-05)[:, None]
         query = (total[:, :query_cols] * inv).astype(bf16)
-        keyval = (total[:, query_cols:] * inv).astype(bf16)
+        keyval = (total[:, query_cols : query_cols + kv_cols] * inv).astype(bf16)
         query_heads = query.reshape(
             slots_local, rounds, DRAFT_BLOCK, kv_local, GROUP_HEADS, HEAD_SIZE
         )
@@ -148,6 +152,13 @@
         by_zy = gather_from(by_z, y_pos, n_y, along_y)
         gathered = by_zy.transpose(1, 0, 2, 3).reshape(-1, query_cols)
         partial = jnp.dot(gathered, w_out[0], preferred_element_type=f32)
+        ext_new = jnp.where(keep[:, None, :, None], fresh, jnp.zeros_like(fresh))
+        if last:
+            natural = jnp.take(partial.astype(bf16), back_index, axis=0)
+            pieces = natural.reshape(rounds, n_tensor, rows_local, width_local).transpose(1, 0, 2, 3)
+            mine = sum(r.astype(f32) for r in spread(pieces, tensor, along_tensor))
+            x_own = jnp.take(xf, own_index, axis=0).reshape(rounds, rows_local, width_local)
+            return None, (x_own + mine).astype(bf16), ext_new
         quarter = partial.shape[0] // n_tensor
         pieces = partial.astype(bf16).reshape(n_tensor, quarter, width_local)
         mine = sum(r.astype(f32) for r in spread(pieces, tensor, along_tensor))
@@ -156,8 +167,8 @@
         )
         x_mine = (x_mine + mine).astype(bf16)
         x_new = gather_from(x_mine, tensor, n_tensor, along_tensor).reshape(-1, width_local)
-        ext_new = jnp.where(keep[:, None, :, None], fresh, jnp.zeros_like(fresh))
-        return x_new, ext_new
+        rec_new = jnp.take(x_new, own_index, axis=0).reshape(rounds, rows_local, width_local)
+        return x_new, rec_new, ext_new
 
     rows_all = gather_from(hidden, tensor, n_tensor, along_tensor)
     rows_all = rows_all.transpose(1, 0, 2, 3).reshape(-1, width_local)
@@ -165,8 +176,7 @@
     record = None
     ext = None
     for step in range(n_segment):
-        x_new, ext_new = layer(x)
-        rec_new = jnp.take(x_new, own_index, axis=0).reshape(rounds, rows_local, width_local)
+        x_new, rec_new, ext_new = layer(x, step + 1 == n_segment)
         if step == 0:
             record, ext = rec_new, ext_new
         else:

time: 257 us -> 249 us (0.969)
  starting transfers between devices: 76.2 us -> 50.4 us
  local copies, waits for them, and re-layouts: 19.1 us -> 33.3 us
  other arithmetic: 20.3 us -> 23.3 us
    ppermute x51 -> x36, starting transfers between devices: 74.8 us -> 49 us  [shifted(): return lax.ppermute(x, axis, [(i, fn(i, n)) for i in range(n)])]
    concatenate x0 -> x2, local copies, waits for them, and re-layouts: none -> 6.89 us  [layer(): jnp.concatenate([first.astype(bf16), second.astype(bf16), sq_hi, sq_lo],...]
    squeeze x6, local copies, waits for them, and re-layouts: 1.04 us -> 5.06 us  [spread(): piece = lax.dynamic_index_in_dim(blocks, (pos + k) % m, 0, keepdims=False)]
    squeeze x2 -> x0, other arithmetic: 3.35 us -> none  [spread(): piece = lax.dynamic_index_in_dim(blocks, (pos + k) % m, 0, keepdims=False)]
    convert_element_type x0 -> x4, local copies, waits for them, and re-layouts: none -> 2.66 us  [the longest x2 1.64 us: layer(): sq_hi = sq.astype(bf16)]
    ppermute x51 -> x36, waiting for transfers between devices: 122 us -> 121 us  [shifted(): return lax.ppermute(x, axis, [(i, fn(i, n)) for i in range(n)])]
    gather x7 -> x6, local copies, waits for them, and re-layouts: 6.57 us -> 5.69 us  [gather_from(): return jnp.take(jnp.stack(out), order, axis=0)]
  transfers between devices with their start and end apart: 52 -> 37, of which waited for: 32 -> 24; matrix products, arithmetic and copies ran while one was open for 4% -> 5% of each run, Pallas kernels for 0% -> 0%
where the time goes in v3:
time: 249 us; the launch traced here: 248 us
  waiting for transfers between devices  122 us (49%)
  starting transfers between devices  50.4 us (20%)
  local copies, waits for them, and re-layouts  33.3 us (13%)
  other arithmetic  23.3 us (9%)
  matrix products  17.7 us (7%)
    ppermute x36, waiting for transfers between devices, shifted(): return lax.ppermute(x, axis, [(i, fn(i, n)) for i in range(n)])  121 us
    ppermute x36, starting transfers between devices, shifted(): return lax.ppermute(x, axis, [(i, fn(i, n)) for i in range(n)])  49 us
    dot_general x2, matrix products, layer(): first = jnp.dot(xg, w_query[0], preferred_element_type=f32)  10.4 us
    concatenate x2, local copies, waits for them, and re-layouts, layer(): jnp.concatenate([first.astype(bf16), second.astype(bf16), sq_hi, sq_lo],...  6.89 us
    gather x6, local copies, waits for them, and re-layouts, gather_from(): return jnp.take(jnp.stack(out), order, axis=0)  5.69 us
    add x2, other arithmetic, layer(): part = sum((r.astype(f32) for r in spread(by_y, y_pos, along_y)))  5.17 us
    squeeze x6, local copies, waits for them, and re-layouts, spread(): piece = lax.dynamic_index_in_dim(blocks, (pos + k) % m, 0, keepdims=False)  5.06 us
  transfers between devices with their start and end apart: 37, of which 24 were waited for; matrix products, arithmetic and copies ran while one was open for 5% of the time, Pallas kernels for 0%

profile of v3, /device:TPU:0, one launch (start us, length us, event | category | flops | bytes accessed | tf_op | source)
XLA Modules:
  0.0 248.4 jit_solution(16332702660986795087)
XLA Ops:
  20.8 5.3 %fusion.8 = bf16[384,2048]{1,0:T(8,128)(2,1)} fusion(bf16[1,1024,2048]{2,1,0:T(8,128)(2,1)} %param.16, f32[1024]{0:T(1024)S(1)} %bitcast.271, bf16[384,1024]{1,0:T(8,128)(2,1)S(1)} %gather_fusion.6, pred[384]{0:T(512)(128)(4,1)S(1)} %get-tuple-element.48), kind=kOutput, calls=%fused_computation.20 | convolution fusion | flops 1612972032 | bytes 6558080 | tf_op jit(solution)/shard_map/dot_general | solution.py:120
  26.1 3.4 %concatenate.30 = bf16[4,4,24,2562]{3,2,1,0:T(8,128)(2,1)S(1)} concatenate(bf16[4,4,24,2048]{3,2,1,0:T(8,128)(2,1)} %bitcast.230, bf16[4,4,24,512]{3,2,1,0:T(8,128)(2,1)S(1)} %bitcast.252, bf16[4,4,24,1]{3,2,1,0:T(8,128)(2,1)} %copy.70, bf16[4,4,24,1]{3,2,1,0:T(8,128)(2,1)} %copy.71), dimensions={3} | concatenate | bytes 3935232 | tf_op jit(solution)/shard_map/concatenate | solution.py:122
  36.2 9.6 %collective-permute-done.3 = bf16[4,24,2562]{2,1,0:T(8,128)(2,1)} collective-permute-done((bf16[4,24,2562]{2,1,0:T(8,128)(2,1)}, bf16[4,24,2562]{2,1,0:T(8,128)(2,1)}, u32[]{:S(2)}, u32[]{:S(2)}) %collective-permute-start.3) | collective-permute-done | bytes 491936 | tf_op jit(solution)/shard_map/ppermute | solution.py:18
  47.2 9.9 %collective-permute-done.4 = bf16[4,24,2562]{2,1,0:T(8,128)(2,1)} collective-permute-done((bf16[4,24,2562]{2,1,0:T(8,128)(2,1)}, bf16[4,24,2562]{2,1,0:T(8,128)(2,1)}, u32[]{:S(2)}, u32[]{:S(2)}) %collective-permute-start.4) | collective-permute-done | bytes 491936 | tf_op jit(solution)/shard_map/ppermute | solution.py:18
  67.2 4.2 %collective-permute-done.6 = f32[24,2562]{1,0:T(8,128)S(1)} collective-permute-done((f32[24,2562]{1,0:T(8,128)S(1)}, f32[24,2562]{1,0:T(8,128)S(1)}, u32[]{:S(2)}, u32[]{:S(2)}) %collective-permute-start.6) | collective-permute-done | bytes 245984 | tf_op jit(solution)/shard_map/ppermute | solution.py:18
  71.3 3.2 %collective-permute-done.8 = f32[24,2562]{1,0:T(8,128)S(1)} collective-permute-done((f32[24,2562]{1,0:T(8,128)S(1)}, f32[24,2562]{1,0:T(8,128)S(1)}, u32[]{:S(2)}, u32[]{:S(2)}) %collective-permute-start.8) | collective-permute-done | bytes 245984 | tf_op jit(solution)/shard_map/ppermute | solution.py:18
  84.9 2.9 %collective-permute-done.10 = bf16[24,2048]{1,0:T(8,128)(2,1)S(1)} collective-permute-done((bf16[24,2048]{1,0:T(8,128)(2,1)S(1)}, bf16[24,2048]{1,0:T(8,128)(2,1)S(1)}, u32[]{:S(2)}, u32[]{:S(2)}) %collective-permute-start.10) | collective-permute-done | bytes 98336 | tf_op jit(solution)/shard_map/ppermute | solution.py:18
  93.9 7.8 %collective-permute-done.13 = bf16[4,24,2048]{2,1,0:T(8,128)(2,1)S(1)} collective-permute-done((bf16[4,24,2048]{2,1,0:T(8,128)(2,1)S(1)}, bf16[4,24,2048]{2,1,0:T(8,128)(2,1)S(1)}, u32[]{:S(2)}, u32[]{:S(2)}) %collective-permute-start.13) | collective-permute-done | bytes 393248 | tf_op jit(solution)/shard_map/ppermute | solution.py:18
  101.7 4.1 %collective-permute-done.12 = bf16[4,24,2048]{2,1,0:T(8,128)(2,1)S(1)} collective-permute-done((bf16[4,24,2048]{2,1,0:T(8,128)(2,1)S(1)}, bf16[4,24,2048]{2,1,0:T(8,128)(2,1)S(1)}, u32[]{:S(2)}, u32[]{:S(2)}) %collective-permute-start.12) | collective-permute-done | bytes 393248 | tf_op jit(solution)/shard_map/ppermute | solution.py:18
  112.7 2.9 %collective-permute-start.17 = (bf16[96,1024]{1,0:T(8,128)(2,1)S(1)}, bf16[96,1024]{1,0:T(8,128)(2,1)S(1)}, u32[]{:S(2)}, u32[]{:S(2)}) collective-permute-start(bf16[96,1024]{1,0:T(8,128)(2,1)S(1)} %get-tuple-element.33), channel_id=1, source_target_pairs={{0,48},{16,0},{32,16},{48,32},{1,49},{17,1},{33,17},{49,33},{2,50}... | collective-permute-start | bytes 589832 | tf_op jit(solution)/shard_map/ppermute | solution.py:18
  115.8 7.7 %collective-permute-done.15 = bf16[96,1024]{1,0:T(8,128)(2,1)S(1)} collective-permute-done((bf16[96,1024]{1,0:T(8,128)(2,1)S(1)}, bf16[96,1024]{1,0:T(8,128)(2,1)S(1)}, u32[]{:S(2)}, u32[]{:S(2)}) %collective-permute-start.15) | collective-permute-done | bytes 196640 | tf_op jit(solution)/shard_map/ppermute | solution.py:18
  127.0 4.2 %collective-permute-done.20 = bf16[96,1024]{1,0:T(8,128)(2,1)S(1)} collective-permute-done((bf16[96,1024]{1,0:T(8,128)(2,1)S(1)}, bf16[96,1024]{1,0:T(8,128)(2,1)S(1)}, u32[]{:S(2)}, u32[]{:S(2)}) %collective-permute-start.20) | collective-permute-done | bytes 196640 | tf_op jit(solution)/shard_map/ppermute | solution.py:18
  143.7 5.1 %fusion.11 = bf16[384,2048]{1,0:T(8,128)(2,1)} fusion(bf16[1,1024,2048]{2,1,0:T(8,128)(2,1)} %param.16, bf16[384,1024]{1,0:T(8,128)(2,1)S(1)} %collective-permute-done.21, f32[1024]{0:T(1024)S(1)} %bitcast.273), kind=kOutput, calls=%fused_computation.21 | convolution fusion | flops 1612578816 | bytes 6557696 | tf_op jit(solution)/shard_map/dot_general | solution.py:120
  148.8 3.5 %concatenate.35 = bf16[4,4,24,2562]{3,2,1,0:T(8,128)(2,1)S(1)} concatenate(bf16[4,4,24,2048]{3,2,1,0:T(8,128)(2,1)} %bitcast.229, bf16[4,4,24,512]{3,2,1,0:T(8,128)(2,1)} %bitcast.251, bf16[4,4,24,1]{3,2,1,0:T(8,128)(2,1)} %copy.79, bf16[4,4,24,1]{3,2,1,0:T(8,128)(2,1)S(1)} %copy.80), dimensions={3} | concatenate | bytes 3935232 | tf_op jit(solution)/shard_map/concatenate | solution.py:122
  153.5 3.2 %collective-permute-start.24 = (bf16[4,24,2562]{2,1,0:T(8,128)(2,1)}, bf16[4,24,2562]{2,1,0:T(8,128)(2,1)}, u32[]{:S(2)}, u32[]{:S(2)}) collective-permute-start(bf16[4,24,2562]{2,1,0:T(8,128)(2,1)} %get-tuple-element.18), channel_id=1, source_target_pairs={{0,3},{1,0},{2,1},{3,2},{4,7},{5,4},{6,5},{7,6},{8,11},{9,8},{10,9... | collective-permute-start | bytes 1475720 | tf_op jit(solution)/shard_map/ppermute | solution.py:18
  157.0 23.1 %collective-permute-done.22 = bf16[4,24,2562]{2,1,0:T(8,128)(2,1)} collective-permute-done((bf16[4,24,2562]{2,1,0:T(8,128)(2,1)}, bf16[4,24,2562]{2,1,0:T(8,128)(2,1)}, u32[]{:S(2)}, u32[]{:S(2)}) %collective-permute-start.22) | collective-permute-done | bytes 491936 | tf_op jit(solution)/shard_map/ppermute | solution.py:18
  184.5 2.7 %collective-permute-start.27 = (f32[24,2562]{1,0:T(8,128)S(1)}, f32[24,2562]{1,0:T(8,128)S(1)}, u32[]{:S(2)}, u32[]{:S(2)}) collective-permute-start(f32[24,2562]{1,0:T(8,128)S(1)} %get-tuple-element.24), channel_id=1, source_target_pairs={{0,12},{1,13},{2,14},{3,15},{4,0},{5,1},{6,2},{7,3},{8,4},{9,5},{1... | collective-permute-start | bytes 737864 | tf_op jit(solution)/shard_map/ppermute | solution.py:18
  188.7 9.7 %collective-permute-done.25 = f32[24,2562]{1,0:T(8,128)S(1)} collective-permute-done((f32[24,2562]{1,0:T(8,128)S(1)}, f32[24,2562]{1,0:T(8,128)S(1)}, u32[]{:S(2)}, u32[]{:S(2)}) %collective-permute-start.25) | collective-permute-done | bytes 245984 | tf_op jit(solution)/shard_map/ppermute | solution.py:18
  201.1 3.0 %collective-permute-start.30 = (bf16[24,2048]{1,0:T(8,128)(2,1)S(1)}, bf16[24,2048]{1,0:T(8,128)(2,1)S(1)}, u32[]{:S(2)}, u32[]{:S(2)}) collective-permute-start(bf16[24,2048]{1,0:T(8,128)(2,1)S(1)} %reshape.633), channel_id=1, source_target_pairs={{0,12},{1,13},{2,14},{3,15},{4,0},{5,1},{6,2},{7,3},{8,4},{9,5},{1... | collective-permute-start | bytes 294920 | tf_op jit(solution)/shard_map/ppermute | solution.py:18
  212.7 2.7 %collective-permute-start.31 = (bf16[4,24,2048]{2,1,0:T(8,128)(2,1)S(1)}, bf16[4,24,2048]{2,1,0:T(8,128)(2,1)S(1)}, u32[]{:S(2)}, u32[]{:S(2)}) collective-permute-start(bf16[4,24,2048]{2,1,0:T(8,128)(2,1)S(1)} %broadcast_select_fusion.1), channel_id=1, source_target_pairs={{0,1},{1,2},{2,3},{3,0},{4,5},{5,6},{6,7},{7,4},{8,9},{9,10},{10,1... | collective-permute-start | bytes 1179656 | tf_op jit(solution)/shard_map/ppermute | solution.py:18
  216.1 8.6 %collective-permute-done.32 = bf16[4,24,2048]{2,1,0:T(8,128)(2,1)S(1)} collective-permute-done((bf16[4,24,2048]{2,1,0:T(8,128)(2,1)S(1)}, bf16[4,24,2048]{2,1,0:T(8,128)(2,1)S(1)}, u32[]{:S(2)}, u32[]{:S(2)}) %collective-permute-start.32) | collective-permute-done | bytes 393248 | tf_op jit(solution)/shard_map/ppermute | solution.py:18
  224.7 4.2 %collective-permute-done.31 = bf16[4,24,2048]{2,1,0:T(8,128)(2,1)S(1)} collective-permute-done((bf16[4,24,2048]{2,1,0:T(8,128)(2,1)S(1)}, bf16[4,24,2048]{2,1,0:T(8,128)(2,1)S(1)}, u32[]{:S(2)}, u32[]{:S(2)}) %collective-permute-start.31) | collective-permute-done | bytes 393248 | tf_op jit(solution)/shard_map/ppermute | solution.py:18
  236.2 3.2 %collective-permute-start.36 = (bf16[3,32,1024]{2,1,0:T(8,128)(2,1)S(1)}, bf16[3,32,1024]{2,1,0:T(8,128)(2,1)S(1)}, u32[]{:S(2)}, u32[]{:S(2)}) collective-permute-start(bf16[3,32,1024]{2,1,0:T(8,128)(2,1)S(1)} %get-tuple-element.30), channel_id=1, source_target_pairs={{0,48},{16,0},{32,16},{48,32},{1,49},{17,1},{33,17},{49,33},{2,50}... | collective-permute-start | bytes 589832 | tf_op jit(solution)/shard_map/ppermute | solution.py:18
  240.1 7.3 %collective-permute-done.34 = bf16[3,32,1024]{2,1,0:T(8,128)(2,1)S(1)} collective-permute-done((bf16[3,32,1024]{2,1,0:T(8,128)(2,1)S(1)}, bf16[3,32,1024]{2,1,0:T(8,128)(2,1)S(1)}, u32[]{:S(2)}, u32[]{:S(2)}) %collective-permute-start.34) | collective-permute-done | bytes 196640 | tf_op jit(solution)/shard_map/ppermute | solution.py:18
  (240 shorter events, 105.1 us)
Async XLA Ops:
  0.6 11.3 %collective-permute-start = (bf16[3,32,1024]{2,1,0:T(8,128)(2,1)}, bf16[3,32,1024]{2,1,0:T(8,128)(2,1)S(1)}, u32[]{:S(2)}, u32[]{:S(2)}) collective-permute-start(bf16[3,32,1024]{2,1,0:T(8,128)(2,1)} %param.14), channel_id=1, source_target_pairs={{0,16},{16,32},{32,48},{48,0},{1,17},{17,33},{33,49},{49,1},{2,18}... | collective-permute-start | bytes 589832 | tf_op jit(solution)/shard_map/ppermute | solution.py:18
  4.0 10.1 %collective-permute-start.1 = (bf16[3,32,1024]{2,1,0:T(8,128)(2,1)}, bf16[3,32,1024]{2,1,0:T(8,128)(2,1)S(1)}, u32[]{:S(2)}, u32[]{:S(2)}) collective-permute-start(bf16[3,32,1024]{2,1,0:T(8,128)(2,1)} %param.14), channel_id=1, source_target_pairs={{0,32},{16,48},{32,0},{48,16},{1,33},{17,49},{33,1},{49,17},{2,34}... | collective-permute-start | bytes 589832 | tf_op jit(solution)/shard_map/ppermute | solution.py:18
  30.7 15.0 %collective-permute-start.3 = (bf16[4,24,2562]{2,1,0:T(8,128)(2,1)}, bf16[4,24,2562]{2,1,0:T(8,128)(2,1)}, u32[]{:S(2)}, u32[]{:S(2)}) collective-permute-start(bf16[4,24,2562]{2,1,0:T(8,128)(2,1)} %get-tuple-element.20), channel_id=1, source_target_pairs={{0,1},{1,2},{2,3},{3,0},{4,5},{5,6},{6,7},{7,4},{8,9},{9,10},{10,1... | collective-permute-start | bytes 1475720 | tf_op jit(solution)/shard_map/ppermute | solution.py:18
  32.3 14.9 %collective-permute-start.5 = (bf16[4,24,2562]{2,1,0:T(8,128)(2,1)}, bf16[4,24,2562]{2,1,0:T(8,128)(2,1)}, u32[]{:S(2)}, u32[]{:S(2)}) collective-permute-start(bf16[4,24,2562]{2,1,0:T(8,128)(2,1)} %get-tuple-element.21), channel_id=1, source_target_pairs={{0,3},{1,0},{2,1},{3,2},{4,7},{5,4},{6,5},{7,6},{8,11},{9,8},{10,9... | collective-permute-start | bytes 1475720 | tf_op jit(solution)/shard_map/ppermute | solution.py:18
  34.0 23.2 %collective-permute-start.4 = (bf16[4,24,2562]{2,1,0:T(8,128)(2,1)}, bf16[4,24,2562]{2,1,0:T(8,128)(2,1)}, u32[]{:S(2)}, u32[]{:S(2)}) collective-permute-start(bf16[4,24,2562]{2,1,0:T(8,128)(2,1)} %get-tuple-element.22), channel_id=1, source_target_pairs={{0,2},{1,3},{2,0},{3,1},{4,6},{5,7},{6,4},{7,5},{8,10},{9,11},{10,... | collective-permute-start | bytes 1475720 | tf_op jit(solution)/shard_map/ppermute | solution.py:18
  61.1 10.3 %collective-permute-start.6 = (f32[24,2562]{1,0:T(8,128)S(1)}, f32[24,2562]{1,0:T(8,128)S(1)}, u32[]{:S(2)}, u32[]{:S(2)}) collective-permute-start(f32[24,2562]{1,0:T(8,128)S(1)} %get-tuple-element.26), channel_id=1, source_target_pairs={{0,4},{1,5},{2,6},{3,7},{4,8},{5,9},{6,10},{7,11},{8,12},{9,13},{1... | collective-permute-start | bytes 737864 | tf_op jit(solution)/shard_map/ppermute | solution.py:18
  63.1 11.5 %collective-permute-start.8 = (f32[24,2562]{1,0:T(8,128)S(1)}, f32[24,2562]{1,0:T(8,128)S(1)}, u32[]{:S(2)}, u32[]{:S(2)}) collective-permute-start(f32[24,2562]{1,0:T(8,128)S(1)} %get-tuple-element.27), channel_id=1, source_target_pairs={{0,12},{1,13},{2,14},{3,15},{4,0},{5,1},{6,2},{7,3},{8,4},{9,5},{1... | collective-permute-start | bytes 737864 | tf_op jit(solution)/shard_map/ppermute | solution.py:18
  65.3 11.2 %collective-permute-start.7 = (f32[24,2562]{1,0:T(8,128)S(1)}, f32[24,2562]{1,0:T(8,128)}, u32[]{:S(2)}, u32[]{:S(2)}) collective-permute-start(f32[24,2562]{1,0:T(8,128)S(1)} %get-tuple-element.28), channel_id=1, source_target_pairs={{0,8},{1,9},{2,10},{3,11},{4,12},{5,13},{6,14},{7,15},{8,0},{9,1},... | collective-permute-start | bytes 737864 | tf_op jit(solution)/shard_map/ppermute | solution.py:18
  89.7 11.9 %collective-permute-start.13 = (bf16[4,24,2048]{2,1,0:T(8,128)(2,1)S(1)}, bf16[4,24,2048]{2,1,0:T(8,128)(2,1)S(1)}, u32[]{:S(2)}, u32[]{:S(2)}) collective-permute-start(bf16[4,24,2048]{2,1,0:T(8,128)(2,1)S(1)} %broadcast_select_fusion.2), channel_id=1, source_target_pairs={{0,2},{1,3},{2,0},{3,1},{4,6},{5,7},{6,4},{7,5},{8,10},{9,11},{10,... | collective-permute-start | bytes 1179656 | tf_op jit(solution)/shard_map/ppermute | solution.py:18
  90.5 15.2 %collective-permute-start.12 = (bf16[4,24,2048]{2,1,0:T(8,128)(2,1)S(1)}, bf16[4,24,2048]{2,1,0:T(8,128)(2,1)S(1)}, u32[]{:S(2)}, u32[]{:S(2)}) collective-permute-start(bf16[4,24,2048]{2,1,0:T(8,128)(2,1)S(1)} %broadcast_select_fusion.2), channel_id=1, source_target_pairs={{0,1},{1,2},{2,3},{3,0},{4,5},{5,6},{6,7},{7,4},{8,9},{9,10},{10,1... | collective-permute-start | bytes 1179656 | tf_op jit(solution)/shard_map/ppermute | solution.py:18
  92.0 13.7 %collective-permute-start.14 = (bf16[4,24,2048]{2,1,0:T(8,128)(2,1)S(1)}, bf16[4,24,2048]{2,1,0:T(8,128)(2,1)S(1)}, u32[]{:S(2)}, u32[]{:S(2)}) collective-permute-start(bf16[4,24,2048]{2,1,0:T(8,128)(2,1)S(1)} %broadcast_select_fusion.2), channel_id=1, source_target_pairs={{0,3},{1,0},{2,1},{3,2},{4,7},{5,4},{6,5},{7,6},{8,11},{9,8},{10,9... | collective-permute-start | bytes 1179656 | tf_op jit(solution)/shard_map/ppermute | solution.py:18
  112.3 11.2 %collective-permute-start.15 = (bf16[96,1024]{1,0:T(8,128)(2,1)S(1)}, bf16[96,1024]{1,0:T(8,128)(2,1)S(1)}, u32[]{:S(2)}, u32[]{:S(2)}) collective-permute-start(bf16[96,1024]{1,0:T(8,128)(2,1)S(1)} %get-tuple-element.32), channel_id=1, source_target_pairs={{0,16},{16,32},{32,48},{48,0},{1,17},{17,33},{33,49},{49,1},{2,18}... | collective-permute-start | bytes 589832 | tf_op jit(solution)/shard_map/ppermute | solution.py:18
  112.7 10.8 %collective-permute-start.17 = (bf16[96,1024]{1,0:T(8,128)(2,1)S(1)}, bf16[96,1024]{1,0:T(8,128)(2,1)S(1)}, u32[]{:S(2)}, u32[]{:S(2)}) collective-permute-start(bf16[96,1024]{1,0:T(8,128)(2,1)S(1)} %get-tuple-element.33), channel_id=1, source_target_pairs={{0,48},{16,0},{32,16},{48,32},{1,49},{17,1},{33,17},{49,33},{2,50}... | collective-permute-start | bytes 589832 | tf_op jit(solution)/shard_map/ppermute | solution.py:18
  153.5 26.6 %collective-permute-start.22 = (bf16[4,24,2562]{2,1,0:T(8,128)(2,1)}, bf16[4,24,2562]{2,1,0:T(8,128)(2,1)}, u32[]{:S(2)}, u32[]{:S(2)}) collective-permute-start(bf16[4,24,2562]{2,1,0:T(8,128)(2,1)} %get-tuple-element.17), channel_id=1, source_target_pairs={{0,1},{1,2},{2,3},{3,0},{4,5},{5,6},{6,7},{7,4},{8,9},{9,10},{10,1... | collective-permute-start | bytes 1475720 | tf_op jit(solution)/shard_map/ppermute | solution.py:18
  153.5 26.6 %collective-permute-start.24 = (bf16[4,24,2562]{2,1,0:T(8,128)(2,1)}, bf16[4,24,2562]{2,1,0:T(8,128)(2,1)}, u32[]{:S(2)}, u32[]{:S(2)}) collective-permute-start(bf16[4,24,2562]{2,1,0:T(8,128)(2,1)} %get-tuple-element.18), channel_id=1, source_target_pairs={{0,3},{1,0},{2,1},{3,2},{4,7},{5,4},{6,5},{7,6},{8,11},{9,8},{10,9... | collective-permute-start | bytes 1475720 | tf_op jit(solution)/shard_map/ppermute | solution.py:18
  156.7 23.4 %collective-permute-start.23 = (bf16[4,24,2562]{2,1,0:T(8,128)(2,1)}, bf16[4,24,2562]{2,1,0:T(8,128)(2,1)}, u32[]{:S(2)}, u32[]{:S(2)}) collective-permute-start(bf16[4,24,2562]{2,1,0:T(8,128)(2,1)} %get-tuple-element.19), channel_id=1, source_target_pairs={{0,2},{1,3},{2,0},{3,1},{4,6},{5,7},{6,4},{7,5},{8,10},{9,11},{10,... | collective-permute-start | bytes 1475720 | tf_op jit(solution)/shard_map/ppermute | solution.py:18
  183.9 14.5 %collective-permute-start.25 = (f32[24,2562]{1,0:T(8,128)S(1)}, f32[24,2562]{1,0:T(8,128)S(1)}, u32[]{:S(2)}, u32[]{:S(2)}) collective-permute-start(f32[24,2562]{1,0:T(8,128)S(1)} %get-tuple-element.23), channel_id=1, source_target_pairs={{0,4},{1,5},{2,6},{3,7},{4,8},{5,9},{6,10},{7,11},{8,12},{9,13},{1... | collective-permute-start | bytes 737864 | tf_op jit(solution)/shard_map/ppermute | solution.py:18
  184.5 13.9 %collective-permute-start.27 = (f32[24,2562]{1,0:T(8,128)S(1)}, f32[24,2562]{1,0:T(8,128)S(1)}, u32[]{:S(2)}, u32[]{:S(2)}) collective-permute-start(f32[24,2562]{1,0:T(8,128)S(1)} %get-tuple-element.24), channel_id=1, source_target_pairs={{0,12},{1,13},{2,14},{3,15},{4,0},{5,1},{6,2},{7,3},{8,4},{9,5},{1... | collective-permute-start | bytes 737864 | tf_op jit(solution)/shard_map/ppermute | solution.py:18
  187.2 11.2 %collective-permute-start.26 = (f32[24,2562]{1,0:T(8,128)S(1)}, f32[24,2562]{1,0:T(8,128)S(1)}, u32[]{:S(2)}, u32[]{:S(2)}) collective-permute-start(f32[24,2562]{1,0:T(8,128)S(1)} %get-tuple-element.25), channel_id=1, source_target_pairs={{0,8},{1,9},{2,10},{3,11},{4,12},{5,13},{6,14},{7,15},{8,0},{9,1},... | collective-permute-start | bytes 737864 | tf_op jit(solution)/shard_map/ppermute | solution.py:18
  211.8 12.9 %collective-permute-start.32 = (bf16[4,24,2048]{2,1,0:T(8,128)(2,1)S(1)}, bf16[4,24,2048]{2,1,0:T(8,128)(2,1)S(1)}, u32[]{:S(2)}, u32[]{:S(2)}) collective-permute-start(bf16[4,24,2048]{2,1,0:T(8,128)(2,1)S(1)} %broadcast_select_fusion.1), channel_id=1, source_target_pairs={{0,2},{1,3},{2,0},{3,1},{4,6},{5,7},{6,4},{7,5},{8,10},{9,11},{10,... | collective-permute-start | bytes 1179656 | tf_op jit(solution)/shard_map/ppermute | solution.py:18
  212.7 16.1 %collective-permute-start.31 = (bf16[4,24,2048]{2,1,0:T(8,128)(2,1)S(1)}, bf16[4,24,2048]{2,1,0:T(8,128)(2,1)S(1)}, u32[]{:S(2)}, u32[]{:S(2)}) collective-permute-start(bf16[4,24,2048]{2,1,0:T(8,128)(2,1)S(1)} %broadcast_select_fusion.1), channel_id=1, source_target_pairs={{0,1},{1,2},{2,3},{3,0},{4,5},{5,6},{6,7},{7,4},{8,9},{9,10},{10,1... | collective-permute-start | bytes 1179656 | tf_op jit(solution)/shard_map/ppermute | solution.py:18
  215.4 13.4 %collective-permute-start.33 = (bf16[4,24,2048]{2,1,0:T(8,128)(2,1)S(1)}, bf16[4,24,2048]{2,1,0:T(8,128)(2,1)S(1)}, u32[]{:S(2)}, u32[]{:S(2)}) collective-permute-start(bf16[4,24,2048]{2,1,0:T(8,128)(2,1)S(1)} %broadcast_select_fusion.1), channel_id=1, source_target_pairs={{0,3},{1,0},{2,1},{3,2},{4,7},{5,4},{6,5},{7,6},{8,11},{9,8},{10,9... | collective-permute-start | bytes 1179656 | tf_op jit(solution)/shard_map/ppermute | solution.py:18
  236.1 11.4 %collective-permute-start.34 = (bf16[3,32,1024]{2,1,0:T(8,128)(2,1)S(1)}, bf16[3,32,1024]{2,1,0:T(8,128)(2,1)S(1)}, u32[]{:S(2)}, u32[]{:S(2)}) collective-permute-start(bf16[3,32,1024]{2,1,0:T(8,128)(2,1)S(1)} %get-tuple-element.29), channel_id=1, source_target_pairs={{0,16},{16,32},{32,48},{48,0},{1,17},{17,33},{33,49},{49,1},{2,18}... | collective-permute-start | bytes 589832 | tf_op jit(solution)/shard_map/ppermute | solution.py:18
  236.2 11.3 %collective-permute-start.36 = (bf16[3,32,1024]{2,1,0:T(8,128)(2,1)S(1)}, bf16[3,32,1024]{2,1,0:T(8,128)(2,1)S(1)}, u32[]{:S(2)}, u32[]{:S(2)}) collective-permute-start(bf16[3,32,1024]{2,1,0:T(8,128)(2,1)S(1)} %get-tuple-element.30), channel_id=1, source_target_pairs={{0,48},{16,0},{32,16},{48,32},{1,49},{17,1},{33,17},{49,33},{2,50}... | collective-permute-start | bytes 589832 | tf_op jit(solution)/shard_map/ppermute | solution.py:18
  (36 other events, 256.0 us)

commit v4 on v3

--- a/solution.py
+++ b/solution.py
@@ -13,23 +13,28 @@
 BATCH_INNER = 4
 
 
-def shifted(x, axis, fn):
+def shifted(x, axis, fn, active):
     n = lax.axis_size(axis)
-    return lax.ppermute(x, axis, [(i, fn(i, n)) for i in range(n)])
-
-
-def along_tensor(x, k):
-    return shifted(x, "tensor", lambda i, n: (i + k) % n)
-
-
-def along_y(x, k):
+    pairs = [(active * n + i, active * n + fn(i, n)) for i in range(n)]
+    return lax.ppermute(x, ("segment", axis), pairs)
+
+
+def along_tensor(active):
+    return lambda x, k: shifted(x, "tensor", lambda i, n: (i + k) % n, active)
+
+
+def along_y(active):
     m = BATCH_INNER
-    return shifted(x, "batch", lambda i, n: (i // m) * m + (i % m + k) % m)
-
-
-def along_z(x, k):
+    return lambda x, k: shifted(
+        x, "batch", lambda i, n: (i // m) * m + (i % m + k) % m, active
+    )
+
+
+def along_z(active):
     m = BATCH_INNER
-    return shifted(x, "batch", lambda i, n: ((i // m + k) % (n // m)) * m + i % m)
+    return lambda x, k: shifted(
+        x, "batch", lambda i, n: ((i // m + k) % (n // m)) * m + i % m, active
+    )
 
 
 def spread(blocks, pos, send):
@@ -111,7 +116,8 @@
         owner_slot[None, :, None] * block + rr[:, None, None] * DRAFT_BLOCK + jj[None, None, :]
     ).reshape(-1)
 
-    def layer(x_sorted, last):
+    def layer(x_sorted, last, active):
+        send_t, send_y, send_z = along_tensor(active), along_y(active), along_z(active)
         xf = x_sorted.astype(f32)
         sq = jnp.sum(xf * xf, axis=1, keepdims=True)
         sq_hi = sq.astype(bf16)
@@ -122,8 +128,8 @@
         proj = jnp.concatenate([first.astype(bf16), second.astype(bf16), sq_hi, sq_lo], axis=1)
         cols = proj.shape[1]
         by_y = proj.reshape(n_z, n_y, own_rows, cols).transpose(1, 0, 2, 3)
-        part = sum(r.astype(f32) for r in spread(by_y, y_pos, along_y))
-        total = sum(spread(part, z_pos, along_z))
+        part = sum(r.astype(f32) for r in spread(by_y, y_pos, send_y))
+        total = sum(spread(part, z_pos, send_z))
         total_sq = total[:, query_cols + kv_cols] + total[:, query_cols + kv_cols + 1]
         inv = lax.rsqrt(total_sq / MODEL_WIDTH + 1e-05)[:, None]
         query = (total[:, :query_cols] * inv).astype(bf16)
@@ -148,35 +154,35 @@
             "shgrjl,shld->srjhgd", weights, values, preferred_element_type=f32
         )
         attended = attended.astype(bf16).reshape(own_rows, query_cols)
-        by_z = gather_from(attended, z_pos, n_z, along_z)
-        by_zy = gather_from(by_z, y_pos, n_y, along_y)
+        by_z = gather_from(attended, z_pos, n_z, send_z)
+        by_zy = gather_from(by_z, y_pos, n_y, send_y)
         gathered = by_zy.transpose(1, 0, 2, 3).reshape(-1, query_cols)
         partial = jnp.dot(gathered, w_out[0], preferred_element_type=f32)
         ext_new = jnp.where(keep[:, None, :, None], fresh, jnp.zeros_like(fresh))
         if last:
             natural = jnp.take(partial.astype(bf16), back_index, axis=0)
             pieces = natural.reshape(rounds, n_tensor, rows_local, width_local).transpose(1, 0, 2, 3)
-            mine = sum(r.astype(f32) for r in spread(pieces, tensor, along_tensor))
+            mine = sum(r.astype(f32) for r in spread(pieces, tensor, send_t))
             x_own = jnp.take(xf, own_index, axis=0).reshape(rounds, rows_local, width_local)
             return None, (x_own + mine).astype(bf16), ext_new
         quarter = partial.shape[0] // n_tensor
         pieces = partial.astype(bf16).reshape(n_tensor, quarter, width_local)
-        mine = sum(r.astype(f32) for r in spread(pieces, tensor, along_tensor))
+        mine = sum(r.astype(f32) for r in spread(pieces, tensor, send_t))
         x_mine = lax.dynamic_index_in_dim(
             xf.reshape(n_tensor, quarter, width_local), tensor, 0, keepdims=False
         )
         x_mine = (x_mine + mine).astype(bf16)
-        x_new = gather_from(x_mine, tensor, n_tensor, along_tensor).reshape(-1, width_local)
+        x_new = gather_from(x_mine, tensor, n_tensor, send_t).reshape(-1, width_local)
         rec_new = jnp.take(x_new, own_index, axis=0).reshape(rounds, rows_local, width_local)
         return x_new, rec_new, ext_new
 
-    rows_all = gather_from(hidden, tensor, n_tensor, along_tensor)
+    rows_all = gather_from(hidden, tensor, n_tensor, along_tensor(0))
     rows_all = rows_all.transpose(1, 0, 2, 3).reshape(-1, width_local)
     x = jnp.take(rows_all, sort_index, axis=0)
     record = None
     ext = None
     for step in range(n_segment):
-        x_new, rec_new, ext_new = layer(x, step + 1 == n_segment)
+        x_new, rec_new, ext_new = layer(x, step + 1 == n_segment, step)
         if step == 0:
             record, ext = rec_new, ext_new
         else:

time: 249 us -> 261 us (1.048)
  the two profiles are of different devices: /device:TPU:0 before, /device:TPU:1 now
where the time goes in v4:
time: 261 us; the launch traced here: 260 us
  waiting for transfers between devices  120 us (46%)
  starting transfers between devices  63.6 us (24%)
  local copies, waits for them, and re-layouts  33.3 us (13%)
  other arithmetic  23.3 us (9%)
  matrix products  17.7 us (7%)
    ppermute x1, waiting for transfers between devices, passed_along(): return lax.ppermute(block, axis, route)  94.1 us
    ppermute x36, starting transfers between devices, shifted(): return lax.ppermute(x, ('segment', axis), pairs)  62.1 us
    ppermute x36, waiting for transfers between devices, shifted(): return lax.ppermute(x, ('segment', axis), pairs)  25.6 us
    dot_general x2, matrix products, layer(): first = jnp.dot(xg, w_query[0], preferred_element_type=f32)  10.4 us
    concatenate x2, local copies, waits for them, and re-layouts, layer(): jnp.concatenate([first.astype(bf16), second.astype(bf16), sq_hi, sq_lo],...  6.89 us
    gather x6, local copies, waits for them, and re-layouts, gather_from(): return jnp.take(jnp.stack(out), order, axis=0)  5.69 us
  transfers between devices with their start and end apart: 37, of which 9 were waited for; matrix products, arithmetic and copies ran while one was open for 5% of the time, Pallas kernels for 0%

profile of v4, /device:TPU:1, one launch (start us, length us, event | category | flops | bytes accessed | tf_op | source)
XLA Modules:
  0.0 259.7 jit_solution(6491403384275432448)
XLA Ops:
  15.8 5.3 %fusion.8 = bf16[384,2048]{1,0:T(8,128)(2,1)} fusion(bf16[1,1024,2048]{2,1,0:T(8,128)(2,1)} %param.16, f32[1024]{0:T(1024)S(1)} %bitcast.271, bf16[384,1024]{1,0:T(8,128)(2,1)S(1)} %gather_fusion.6, pred[384]{0:T(512)(128)(4,1)S(1)} %get-tuple-element.48), kind=kOutput, calls=%fused_computation.20 | convolution fusion | flops 1612972032 | bytes 6558080 | tf_op jit(solution)/shard_map/dot_general | solution.py:126
  21.0 3.4 %concatenate.30 = bf16[4,4,24,2562]{3,2,1,0:T(8,128)(2,1)S(1)} concatenate(bf16[4,4,24,2048]{3,2,1,0:T(8,128)(2,1)} %bitcast.230, bf16[4,4,24,512]{3,2,1,0:T(8,128)(2,1)S(1)} %bitcast.252, bf16[4,4,24,1]{3,2,1,0:T(8,128)(2,1)} %copy.70, bf16[4,4,24,1]{3,2,1,0:T(8,128)(2,1)} %copy.71), dimensions={3} | concatenate | bytes 3935232 | tf_op jit(solution)/shard_map/concatenate | solution.py:128
  30.2 2.6 fusion.33
  61.9 94.1 %collective-permute-done.21 = bf16[384,1024]{1,0:T(8,128)(2,1)S(1)} collective-permute-done((bf16[384,1024]{1,0:T(8,128)(2,1)S(1)}, bf16[384,1024]{1,0:T(8,128)(2,1)S(1)}, u32[]{:S(2)}, u32[]{:S(2)}) %collective-permute-start.21) | collective-permute-done | bytes 786464 | tf_op jit(solution)/shard_map/ppermute | solution.py:58
  158.8 5.1 %fusion.11 = bf16[384,2048]{1,0:T(8,128)(2,1)} fusion(bf16[1,1024,2048]{2,1,0:T(8,128)(2,1)} %param.16, bf16[384,1024]{1,0:T(8,128)(2,1)S(1)} %collective-permute-done.21, f32[1024]{0:T(1024)S(1)} %bitcast.273), kind=kOutput, calls=%fused_computation.21 | convolution fusion | flops 1612578816 | bytes 6557696 | tf_op jit(solution)/shard_map/dot_general | solution.py:126
  163.9 3.5 %concatenate.35 = bf16[4,4,24,2562]{3,2,1,0:T(8,128)(2,1)S(1)} concatenate(bf16[4,4,24,2048]{3,2,1,0:T(8,128)(2,1)} %bitcast.229, bf16[4,4,24,512]{3,2,1,0:T(8,128)(2,1)} %bitcast.251, bf16[4,4,24,1]{3,2,1,0:T(8,128)(2,1)} %copy.79, bf16[4,4,24,1]{3,2,1,0:T(8,128)(2,1)S(1)} %copy.80), dimensions={3} | concatenate | bytes 3935232 | tf_op jit(solution)/shard_map/concatenate | solution.py:128
  168.6 2.3 collective-permute-start.22
  170.8 4.2 %collective-permute-start.24 = (bf16[4,24,2562]{2,1,0:T(8,128)(2,1)}, bf16[4,24,2562]{2,1,0:T(8,128)(2,1)}, u32[]{:S(2)}, u32[]{:S(2)}) collective-permute-start(bf16[4,24,2562]{2,1,0:T(8,128)(2,1)} %get-tuple-element.18), channel_id=1, source_target_pairs={{64,67},{65,64},{66,65},{67,66},{68,71},{69,68},{70,69},{71,70},{7... | collective-permute-start | bytes 1475720 | tf_op jit(solution)/shard_map/ppermute | solution.py:19
  175.1 3.1 %collective-permute-start.23 = (bf16[4,24,2562]{2,1,0:T(8,128)(2,1)}, bf16[4,24,2562]{2,1,0:T(8,128)(2,1)}, u32[]{:S(2)}, u32[]{:S(2)}) collective-permute-start(bf16[4,24,2562]{2,1,0:T(8,128)(2,1)} %get-tuple-element.19), channel_id=1, source_target_pairs={{64,66},{65,67},{66,64},{67,65},{68,70},{69,71},{70,68},{71,69},{7... | collective-permute-start | bytes 1475720 | tf_op jit(solution)/shard_map/ppermute | solution.py:19
  179.9 7.0 %collective-permute-done.24 = bf16[4,24,2562]{2,1,0:T(8,128)(2,1)} collective-permute-done((bf16[4,24,2562]{2,1,0:T(8,128)(2,1)}, bf16[4,24,2562]{2,1,0:T(8,128)(2,1)}, u32[]{:S(2)}, u32[]{:S(2)}) %collective-permute-start.24) | collective-permute-done | bytes 491936 | tf_op jit(solution)/shard_map/ppermute | solution.py:19
  187.0 2.6 fusion.31
  192.7 4.6 %collective-permute-start.27 = (f32[24,2562]{1,0:T(8,128)S(1)}, f32[24,2562]{1,0:T(8,128)S(1)}, u32[]{:S(2)}, u32[]{:S(2)}) collective-permute-start(f32[24,2562]{1,0:T(8,128)S(1)} %get-tuple-element.24), channel_id=1, source_target_pairs={{64,76},{65,77},{66,78},{67,79},{68,64},{69,65},{70,66},{71,67},{7... | collective-permute-start | bytes 737864 | tf_op jit(solution)/shard_map/ppermute | solution.py:19
  197.3 2.5 collective-permute-start.26
  200.5 2.9 %collective-permute-done.27 = f32[24,2562]{1,0:T(8,128)S(1)} collective-permute-done((f32[24,2562]{1,0:T(8,128)S(1)}, f32[24,2562]{1,0:T(8,128)S(1)}, u32[]{:S(2)}, u32[]{:S(2)}) %collective-permute-start.27) | collective-permute-done | bytes 245984 | tf_op jit(solution)/shard_map/ppermute | solution.py:19
  203.3 2.6 collective-permute-done.26
  208.6 2.5 collective-permute-start.30
  213.1 2.8 %collective-permute-start.28 = (bf16[24,2048]{1,0:T(8,128)(2,1)S(1)}, bf16[24,2048]{1,0:T(8,128)(2,1)S(1)}, u32[]{:S(2)}, u32[]{:S(2)}) collective-permute-start(bf16[24,2048]{1,0:T(8,128)(2,1)S(1)} %reshape.633), channel_id=1, source_target_pairs={{64,68},{65,69},{66,70},{67,71},{68,72},{69,73},{70,74},{71,75},{7... | collective-permute-start | bytes 294920 | tf_op jit(solution)/shard_map/ppermute | solution.py:19
  221.0 2.9 %collective-permute-start.32 = (bf16[4,24,2048]{2,1,0:T(8,128)(2,1)S(1)}, bf16[4,24,2048]{2,1,0:T(8,128)(2,1)S(1)}, u32[]{:S(2)}, u32[]{:S(2)}) collective-permute-start(bf16[4,24,2048]{2,1,0:T(8,128)(2,1)S(1)} %broadcast_select_fusion.1), channel_id=1, source_target_pairs={{64,66},{65,67},{66,64},{67,65},{68,70},{69,71},{70,68},{71,69},{7... | collective-permute-start | bytes 1179656 | tf_op jit(solution)/shard_map/ppermute | solution.py:19
  223.9 4.6 %collective-permute-start.31 = (bf16[4,24,2048]{2,1,0:T(8,128)(2,1)S(1)}, bf16[4,24,2048]{2,1,0:T(8,128)(2,1)S(1)}, u32[]{:S(2)}, u32[]{:S(2)}) collective-permute-start(bf16[4,24,2048]{2,1,0:T(8,128)(2,1)S(1)} %broadcast_select_fusion.1), channel_id=1, source_target_pairs={{64,65},{65,66},{66,67},{67,64},{68,69},{69,70},{70,71},{71,68},{7... | collective-permute-start | bytes 1179656 | tf_op jit(solution)/shard_map/ppermute | solution.py:19
  228.5 2.6 collective-permute-start.33
  231.2 4.0 %collective-permute-done.31 = bf16[4,24,2048]{2,1,0:T(8,128)(2,1)S(1)} collective-permute-done((bf16[4,24,2048]{2,1,0:T(8,128)(2,1)S(1)}, bf16[4,24,2048]{2,1,0:T(8,128)(2,1)S(1)}, u32[]{:S(2)}, u32[]{:S(2)}) %collective-permute-start.31) | collective-permute-done | bytes 393248 | tf_op jit(solution)/shard_map/ppermute | solution.py:19
  246.3 4.6 %collective-permute-start.36 = (bf16[3,32,1024]{2,1,0:T(8,128)(2,1)S(1)}, bf16[3,32,1024]{2,1,0:T(8,128)(2,1)S(1)}, u32[]{:S(2)}, u32[]{:S(2)}) collective-permute-start(bf16[3,32,1024]{2,1,0:T(8,128)(2,1)S(1)} %get-tuple-element.30), channel_id=1, source_target_pairs={{64,112},{80,64},{96,80},{112,96},{65,113},{81,65},{97,81},{113,97... | collective-permute-start | bytes 589832 | tf_op jit(solution)/shard_map/ppermute | solution.py:19
  250.9 2.2 collective-permute-start.35
  253.8 5.0 %collective-permute-done.35 = bf16[3,32,1024]{2,1,0:T(8,128)(2,1)S(1)} collective-permute-done((bf16[3,32,1024]{2,1,0:T(8,128)(2,1)S(1)}, bf16[3,32,1024]{2,1,0:T(8,128)(2,1)S(1)}, u32[]{:S(2)}, u32[]{:S(2)}) %collective-permute-start.35) | collective-permute-done | bytes 196640 | tf_op jit(solution)/shard_map/ppermute | solution.py:19
  (240 shorter events, 80.9 us)
Async XLA Ops:
  0.6 8.4 %collective-permute-start = (bf16[3,32,1024]{2,1,0:T(8,128)(2,1)}, bf16[3,32,1024]{2,1,0:T(8,128)(2,1)S(1)}, u32[]{:S(2)}, u32[]{:S(2)}) collective-permute-start(bf16[3,32,1024]{2,1,0:T(8,128)(2,1)} %param.14), channel_id=1, source_target_pairs={{0,16},{16,32},{32,48},{48,0},{1,17},{17,33},{33,49},{49,1},{2,18}... | collective-permute-start | bytes 589832 | tf_op jit(solution)/shard_map/ppermute | solution.py:19
  1.5 7.6 %collective-permute-start.2 = (bf16[3,32,1024]{2,1,0:T(8,128)(2,1)}, bf16[3,32,1024]{2,1,0:T(8,128)(2,1)S(1)}, u32[]{:S(2)}, u32[]{:S(2)}) collective-permute-start(bf16[3,32,1024]{2,1,0:T(8,128)(2,1)} %param.14), channel_id=1, source_target_pairs={{0,48},{16,0},{32,16},{48,32},{1,49},{17,1},{33,17},{49,33},{2,50}... | collective-permute-start | bytes 589832 | tf_op jit(solution)/shard_map/ppermute | solution.py:19
  2.1 6.9 %collective-permute-start.1 = (bf16[3,32,1024]{2,1,0:T(8,128)(2,1)}, bf16[3,32,1024]{2,1,0:T(8,128)(2,1)S(1)}, u32[]{:S(2)}, u32[]{:S(2)}) collective-permute-start(bf16[3,32,1024]{2,1,0:T(8,128)(2,1)} %param.14), channel_id=1, source_target_pairs={{0,32},{16,48},{32,0},{48,16},{1,33},{17,49},{33,1},{49,17},{2,34}... | collective-permute-start | bytes 589832 | tf_op jit(solution)/shard_map/ppermute | solution.py:19
  25.7 4.5 %collective-permute-start.3 = (bf16[4,24,2562]{2,1,0:T(8,128)(2,1)}, bf16[4,24,2562]{2,1,0:T(8,128)(2,1)}, u32[]{:S(2)}, u32[]{:S(2)}) collective-permute-start(bf16[4,24,2562]{2,1,0:T(8,128)(2,1)} %get-tuple-element.20), channel_id=1, source_target_pairs={{0,1},{1,2},{2,3},{3,0},{4,5},{5,6},{6,7},{7,4},{8,9},{9,10},{10,1... | collective-permute-start | bytes 1475720 | tf_op jit(solution)/shard_map/ppermute | solution.py:19
  27.1 3.1 %collective-permute-start.5 = (bf16[4,24,2562]{2,1,0:T(8,128)(2,1)}, bf16[4,24,2562]{2,1,0:T(8,128)(2,1)}, u32[]{:S(2)}, u32[]{:S(2)}) collective-permute-start(bf16[4,24,2562]{2,1,0:T(8,128)(2,1)} %get-tuple-element.21), channel_id=1, source_target_pairs={{0,3},{1,0},{2,1},{3,2},{4,7},{5,4},{6,5},{7,6},{8,11},{9,8},{10,9... | collective-permute-start | bytes 1475720 | tf_op jit(solution)/shard_map/ppermute | solution.py:19
  34.1 2.9 %collective-permute-start.6 = (f32[24,2562]{1,0:T(8,128)S(1)}, f32[24,2562]{1,0:T(8,128)S(1)}, u32[]{:S(2)}, u32[]{:S(2)}) collective-permute-start(f32[24,2562]{1,0:T(8,128)S(1)} %get-tuple-element.26), channel_id=1, source_target_pairs={{0,4},{1,5},{2,6},{3,7},{4,8},{5,9},{6,10},{7,11},{8,12},{9,13},{1... | collective-permute-start | bytes 737864 | tf_op jit(solution)/shard_map/ppermute | solution.py:19
  52.1 2.4 collective-permute-start.15
  54.7 2.2 collective-permute-start.20
  59.8 96.3 %collective-permute-start.21 = (bf16[384,1024]{1,0:T(8,128)(2,1)S(1)}, bf16[384,1024]{1,0:T(8,128)(2,1)S(1)}, u32[]{:S(2)}, u32[]{:S(2)}) collective-permute-start(bf16[384,1024]{1,0:T(8,128)(2,1)S(1)} %bitcast_select_fusion), channel_id=1, source_target_pairs={{0,64},{1,65},{2,66},{3,67},{4,68},{5,69},{6,70},{7,71},{8,72},{9,... | collective-permute-start | bytes 2359304 | tf_op jit(solution)/shard_map/ppermute | solution.py:58
  168.6 11.4 %collective-permute-start.22 = (bf16[4,24,2562]{2,1,0:T(8,128)(2,1)}, bf16[4,24,2562]{2,1,0:T(8,128)(2,1)}, u32[]{:S(2)}, u32[]{:S(2)}) collective-permute-start(bf16[4,24,2562]{2,1,0:T(8,128)(2,1)} %get-tuple-element.17), channel_id=1, source_target_pairs={{64,65},{65,66},{66,67},{67,64},{68,69},{69,70},{70,71},{71,68},{7... | collective-permute-start | bytes 1475720 | tf_op jit(solution)/shard_map/ppermute | solution.py:19
  170.8 16.1 %collective-permute-start.24 = (bf16[4,24,2562]{2,1,0:T(8,128)(2,1)}, bf16[4,24,2562]{2,1,0:T(8,128)(2,1)}, u32[]{:S(2)}, u32[]{:S(2)}) collective-permute-start(bf16[4,24,2562]{2,1,0:T(8,128)(2,1)} %get-tuple-element.18), channel_id=1, source_target_pairs={{64,67},{65,64},{66,65},{67,66},{68,71},{69,68},{70,69},{71,70},{7... | collective-permute-start | bytes 1475720 | tf_op jit(solution)/shard_map/ppermute | solution.py:19
  175.1 11.9 %collective-permute-start.23 = (bf16[4,24,2562]{2,1,0:T(8,128)(2,1)}, bf16[4,24,2562]{2,1,0:T(8,128)(2,1)}, u32[]{:S(2)}, u32[]{:S(2)}) collective-permute-start(bf16[4,24,2562]{2,1,0:T(8,128)(2,1)} %get-tuple-element.19), channel_id=1, source_target_pairs={{64,66},{65,67},{66,64},{67,65},{68,70},{69,71},{70,68},{71,69},{7... | collective-permute-start | bytes 1475720 | tf_op jit(solution)/shard_map/ppermute | solution.py:19
  190.8 9.7 %collective-permute-start.25 = (f32[24,2562]{1,0:T(8,128)S(1)}, f32[24,2562]{1,0:T(8,128)S(1)}, u32[]{:S(2)}, u32[]{:S(2)}) collective-permute-start(f32[24,2562]{1,0:T(8,128)S(1)} %get-tuple-element.23), channel_id=1, source_target_pairs={{64,68},{65,69},{66,70},{67,71},{68,72},{69,73},{70,74},{71,75},{7... | collective-permute-start | bytes 737864 | tf_op jit(solution)/shard_map/ppermute | solution.py:19
  192.7 10.6 %collective-permute-start.27 = (f32[24,2562]{1,0:T(8,128)S(1)}, f32[24,2562]{1,0:T(8,128)S(1)}, u32[]{:S(2)}, u32[]{:S(2)}) collective-permute-start(f32[24,2562]{1,0:T(8,128)S(1)} %get-tuple-element.24), channel_id=1, source_target_pairs={{64,76},{65,77},{66,78},{67,79},{68,64},{69,65},{70,66},{71,67},{7... | collective-permute-start | bytes 737864 | tf_op jit(solution)/shard_map/ppermute | solution.py:19
  197.3 8.6 %collective-permute-start.26 = (f32[24,2562]{1,0:T(8,128)S(1)}, f32[24,2562]{1,0:T(8,128)S(1)}, u32[]{:S(2)}, u32[]{:S(2)}) collective-permute-start(f32[24,2562]{1,0:T(8,128)S(1)} %get-tuple-element.25), channel_id=1, source_target_pairs={{64,72},{65,73},{66,74},{67,75},{68,76},{69,77},{70,78},{71,79},{7... | collective-permute-start | bytes 737864 | tf_op jit(solution)/shard_map/ppermute | solution.py:19
  208.6 10.8 %collective-permute-start.30 = (bf16[24,2048]{1,0:T(8,128)(2,1)S(1)}, bf16[24,2048]{1,0:T(8,128)(2,1)S(1)}, u32[]{:S(2)}, u32[]{:S(2)}) collective-permute-start(bf16[24,2048]{1,0:T(8,128)(2,1)S(1)} %reshape.633), channel_id=1, source_target_pairs={{64,76},{65,77},{66,78},{67,79},{68,64},{69,65},{70,66},{71,67},{7... | collective-permute-start | bytes 294920 | tf_op jit(solution)/shard_map/ppermute | solution.py:19
  211.1 8.3 %collective-permute-start.29 = (bf16[24,2048]{1,0:T(8,128)(2,1)S(1)}, bf16[24,2048]{1,0:T(8,128)(2,1)S(1)}, u32[]{:S(2)}, u32[]{:S(2)}) collective-permute-start(bf16[24,2048]{1,0:T(8,128)(2,1)S(1)} %reshape.633), channel_id=1, source_target_pairs={{64,72},{65,73},{66,74},{67,75},{68,76},{69,77},{70,78},{71,79},{7... | collective-permute-start | bytes 294920 | tf_op jit(solution)/shard_map/ppermute | solution.py:19
  213.1 7.2 %collective-permute-start.28 = (bf16[24,2048]{1,0:T(8,128)(2,1)S(1)}, bf16[24,2048]{1,0:T(8,128)(2,1)S(1)}, u32[]{:S(2)}, u32[]{:S(2)}) collective-permute-start(bf16[24,2048]{1,0:T(8,128)(2,1)S(1)} %reshape.633), channel_id=1, source_target_pairs={{64,68},{65,69},{66,70},{67,71},{68,72},{69,73},{70,74},{71,75},{7... | collective-permute-start | bytes 294920 | tf_op jit(solution)/shard_map/ppermute | solution.py:19
  221.0 10.2 %collective-permute-start.32 = (bf16[4,24,2048]{2,1,0:T(8,128)(2,1)S(1)}, bf16[4,24,2048]{2,1,0:T(8,128)(2,1)S(1)}, u32[]{:S(2)}, u32[]{:S(2)}) collective-permute-start(bf16[4,24,2048]{2,1,0:T(8,128)(2,1)S(1)} %broadcast_select_fusion.1), channel_id=1, source_target_pairs={{64,66},{65,67},{66,64},{67,65},{68,70},{69,71},{70,68},{71,69},{7... | collective-permute-start | bytes 1179656 | tf_op jit(solution)/shard_map/ppermute | solution.py:19
  223.9 11.3 %collective-permute-start.31 = (bf16[4,24,2048]{2,1,0:T(8,128)(2,1)S(1)}, bf16[4,24,2048]{2,1,0:T(8,128)(2,1)S(1)}, u32[]{:S(2)}, u32[]{:S(2)}) collective-permute-start(bf16[4,24,2048]{2,1,0:T(8,128)(2,1)S(1)} %broadcast_select_fusion.1), channel_id=1, source_target_pairs={{64,65},{65,66},{66,67},{67,64},{68,69},{69,70},{70,71},{71,68},{7... | collective-permute-start | bytes 1179656 | tf_op jit(solution)/shard_map/ppermute | solution.py:19
  228.5 8.5 %collective-permute-start.33 = (bf16[4,24,2048]{2,1,0:T(8,128)(2,1)S(1)}, bf16[4,24,2048]{2,1,0:T(8,128)(2,1)S(1)}, u32[]{:S(2)}, u32[]{:S(2)}) collective-permute-start(bf16[4,24,2048]{2,1,0:T(8,128)(2,1)S(1)} %broadcast_select_fusion.1), channel_id=1, source_target_pairs={{64,67},{65,64},{66,65},{67,66},{68,71},{69,68},{70,69},{71,70},{7... | collective-permute-start | bytes 1179656 | tf_op jit(solution)/shard_map/ppermute | solution.py:19
  244.3 9.6 %collective-permute-start.34 = (bf16[3,32,1024]{2,1,0:T(8,128)(2,1)S(1)}, bf16[3,32,1024]{2,1,0:T(8,128)(2,1)S(1)}, u32[]{:S(2)}, u32[]{:S(2)}) collective-permute-start(bf16[3,32,1024]{2,1,0:T(8,128)(2,1)S(1)} %get-tuple-element.29), channel_id=1, source_target_pairs={{64,80},{80,96},{96,112},{112,64},{65,81},{81,97},{97,113},{113,65... | collective-permute-start | bytes 589832 | tf_op jit(solution)/shard_map/ppermute | solution.py:19
  246.3 7.5 %collective-permute-start.36 = (bf16[3,32,1024]{2,1,0:T(8,128)(2,1)S(1)}, bf16[3,32,1024]{2,1,0:T(8,128)(2,1)S(1)}, u32[]{:S(2)}, u32[]{:S(2)}) collective-permute-start(bf16[3,32,1024]{2,1,0:T(8,128)(2,1)S(1)} %get-tuple-element.30), channel_id=1, source_target_pairs={{64,112},{80,64},{96,80},{112,96},{65,113},{81,65},{97,81},{113,97... | collective-permute-start | bytes 589832 | tf_op jit(solution)/shard_map/ppermute | solution.py:19
  250.9 7.9 %collective-permute-start.35 = (bf16[3,32,1024]{2,1,0:T(8,128)(2,1)S(1)}, bf16[3,32,1024]{2,1,0:T(8,128)(2,1)S(1)}, u32[]{:S(2)}, u32[]{:S(2)}) collective-permute-start(bf16[3,32,1024]{2,1,0:T(8,128)(2,1)S(1)} %get-tuple-element.31), channel_id=1, source_target_pairs={{64,96},{80,112},{96,64},{112,80},{65,97},{81,113},{97,65},{113,81... | collective-permute-start | bytes 589832 | tf_op jit(solution)/shard_map/ppermute | solution.py:19
  (36 other events, 150.8 us)

commit v5 on v3

--- a/solution.py
+++ b/solution.py
@@ -23,13 +23,11 @@
 
 
 def along_y(x, k):
-    m = BATCH_INNER
-    return shifted(x, "batch", lambda i, n: (i // m) * m + (i % m + k) % m)
+    return shifted(x, "by", lambda i, n: (i + k) % n)
 
 
 def along_z(x, k):
-    m = BATCH_INNER
-    return shifted(x, "batch", lambda i, n: ((i // m + k) % (n // m)) * m + i % m)
+    return shifted(x, "bz", lambda i, n: (i + k) % n)
 
 
 def spread(blocks, pos, send):
@@ -61,7 +59,7 @@
     n_segment = lax.axis_size("segment")
     segment = lax.axis_index("segment")
     tensor = lax.axis_index("tensor")
-    group = lax.axis_index("batch")
+    group = lax.axis_index("bz") * lax.axis_size("by") + lax.axis_index("by")
     requests = owner_slot.shape[0]
     rows_total = requests * DRAFT_BLOCK
     slots_local = key_value_cache.shape[1]
@@ -103,7 +101,7 @@
 
     n_tensor = lax.axis_size("tensor")
     n_y = BATCH_INNER
-    n_z = lax.axis_size("batch") // n_y
+    n_z = lax.axis_size("bz")
     z_pos = group // n_y
     y_pos = group % n_y
 
@@ -122,8 +120,8 @@
         proj = jnp.concatenate([first.astype(bf16), second.astype(bf16), sq_hi, sq_lo], axis=1)
         cols = proj.shape[1]
         by_y = proj.reshape(n_z, n_y, own_rows, cols).transpose(1, 0, 2, 3)
-        part = sum(r.astype(f32) for r in spread(by_y, y_pos, along_y))
-        total = sum(spread(part, z_pos, along_z))
+        part = jnp.sum(lax.all_to_all(by_y, "by", 0, 0).astype(f32), axis=0)
+        total = jnp.sum(lax.all_to_all(part, "bz", 0, 0), axis=0)
         total_sq = total[:, query_cols + kv_cols] + total[:, query_cols + kv_cols + 1]
         inv = lax.rsqrt(total_sq / MODEL_WIDTH + 1e-05)[:, None]
         query = (total[:, :query_cols] * inv).astype(bf16)
@@ -156,12 +154,12 @@
         if last:
             natural = jnp.take(partial.astype(bf16), back_index, axis=0)
             pieces = natural.reshape(rounds, n_tensor, rows_local, width_local).transpose(1, 0, 2, 3)
-            mine = sum(r.astype(f32) for r in spread(pieces, tensor, along_tensor))
+            mine = jnp.sum(lax.all_to_all(pieces, "tensor", 0, 0).astype(f32), axis=0)
             x_own = jnp.take(xf, own_index, axis=0).reshape(rounds, rows_local, width_local)
             return None, (x_own + mine).astype(bf16), ext_new
         quarter = partial.shape[0] // n_tensor
         pieces = partial.astype(bf16).reshape(n_tensor, quarter, width_local)
-        mine = sum(r.astype(f32) for r in spread(pieces, tensor, along_tensor))
+        mine = jnp.sum(lax.all_to_all(pieces, "tensor", 0, 0).astype(f32), axis=0)
         x_mine = lax.dynamic_index_in_dim(
             xf.reshape(n_tensor, quarter, width_local), tensor, 0, keepdims=False
         )
@@ -189,15 +187,22 @@
 
 
 def solution(mesh):
+    n_batch = mesh.shape["batch"]
+    inner = BATCH_INNER
+    devices = mesh.devices.reshape(
+        mesh.shape["segment"], mesh.shape["tensor"], n_batch // inner, inner
+    )
+    sub = jax.sharding.Mesh(devices, ("segment", "tensor", "bz", "by"))
+    b = ("bz", "by")
     in_specs = (
-        P(None, "tensor", "batch"),
-        P("segment", "batch"),
-        P("segment", "batch", "tensor"),
-        P("segment", "batch", "tensor"),
-        P("segment", "tensor", "batch"),
-        P("segment", "batch", "tensor", None, None),
+        P(None, "tensor", b),
+        P("segment", b),
+        P("segment", b, "tensor"),
+        P("segment", b, "tensor"),
+        P("segment", "tensor", b),
+        P("segment", b, "tensor", None, None),
         P(),
         P(),
     )
-    out_specs = (P("segment", None, "tensor", "batch"), P("segment", "batch", "tensor", None, None))
-    return jax.shard_map(shards, mesh=mesh, in_specs=in_specs, out_specs=out_specs, check_vma=False)
+    out_specs = (P("segment", None, "tensor", b), P("segment", b, "tensor", None, None))
+    return jax.shard_map(shards, mesh=sub, in_specs=in_specs, out_specs=out_specs, check_vma=False)

time: 249 us -> 258 us (1.036)
  waiting for transfers between devices: 122 us -> 147 us
  other arithmetic: 23.3 us -> 18.4 us
  matrix products: 17.7 us -> 13.4 us
  local copies, waits for them, and re-layouts: 33.3 us -> 29.1 us
    all_to_all x0 -> x6, waiting for transfers between devices: none -> 94 us  [the longest x2 48.9 us: layer(): part = jnp.sum(lax.all_to_all(by_y, 'by', 0, 0).astype(f32), axis=0)]
    ppermute x36 -> x18, waiting for transfers between devices: 121 us -> 50.7 us  [shifted(): return lax.ppermute(x, axis, [(i, fn(i, n)) for i in range(n)])]
    ppermute x36 -> x18, starting transfers between devices: 49 us -> 21.2 us  [shifted(): return lax.ppermute(x, axis, [(i, fn(i, n)) for i in range(n)])]
    all_to_all x0 -> x6, starting transfers between devices: none -> 25.5 us  [the longest x2 9.18 us: layer(): total = jnp.sum(lax.all_to_all(part, 'bz', 0, 0), axis=0)]
    add x4 -> x0, other arithmetic: 7.32 us -> none  [the longest x2 5.17 us: layer(): part = sum((r.astype(f32) for r in spread(by_y, y_pos, along_y)))]
    squeeze x6 -> x0, local copies, waits for them, and re-layouts: 5.06 us -> none  [spread(): piece = lax.dynamic_index_in_dim(blocks, (pos + k) % m, 0, keepdims=False)]
    dot_general x2, matrix products: 10.4 us -> 5.94 us  [layer(): first = jnp.dot(xg, w_query[0], preferred_element_type=f32)]
    reduce_sum x0 -> x6, other arithmetic: none -> 4.09 us  [the longest x2 2.52 us: layer(): part = jnp.sum(lax.all_to_all(by_y, 'by', 0, 0).astype(f32), axis=0)]
  transfers between devices with their start and end apart: 37 -> 25, of which waited for: 24 -> 23; matrix products, arithmetic and copies ran while one was open for 5% -> 4% of each run, Pallas kernels for 0% -> 0%
where the time goes in v5:
time: 258 us; the launch traced here: 257 us
  waiting for transfers between devices  147 us (57%)
  starting transfers between devices  48 us (19%)
  local copies, waits for them, and re-layouts  29.1 us (11%)
  other arithmetic  18.4 us (7%)
  matrix products  13.4 us (5%)
    ppermute x18, waiting for transfers between devices, shifted(): return lax.ppermute(x, axis, [(i, fn(i, n)) for i in range(n)])  50.7 us
    all_to_all x2, waiting for transfers between devices, layer(): part = jnp.sum(lax.all_to_all(by_y, 'by', 0, 0).astype(f32), axis=0)  48.9 us
    all_to_all x2, waiting for transfers between devices, layer(): total = jnp.sum(lax.all_to_all(part, 'bz', 0, 0), axis=0)  27.1 us
    ppermute x18, starting transfers between devices, shifted(): return lax.ppermute(x, axis, [(i, fn(i, n)) for i in range(n)])  21.2 us
    all_to_all x2, waiting for transfers between devices, layer(): mine = jnp.sum(lax.all_to_all(pieces, 'tensor', 0, 0).astype(f32), axis=0)  18 us
    all_to_all x2, starting transfers between devices, layer(): total = jnp.sum(lax.all_to_all(part, 'bz', 0, 0), axis=0)  9.18 us
    all_to_all x2, starting transfers between devices, layer(): part = jnp.sum(lax.all_to_all(by_y, 'by', 0, 0).astype(f32), axis=0)  8.33 us
    all_to_all x2, starting transfers between devices, layer(): mine = jnp.sum(lax.all_to_all(pieces, 'tensor', 0, 0).astype(f32), axis=0)  7.99 us
  transfers between devices with their start and end apart: 25, of which 23 were waited for; matrix products, arithmetic and copies ran while one was open for 4% of the time, Pallas kernels for 0%

profile of v5, /device:TPU:0, one launch (start us, length us, event | category | flops | bytes accessed | tf_op | source)
XLA Modules:
  0.0 257.0 jit_solution(5958911679731832260)
XLA Ops:
  10.3 3.8 %collective-permute-done.1 = bf16[3,32,1024]{2,1,0:T(8,128)(2,1)S(1)} collective-permute-done((bf16[3,32,1024]{2,1,0:T(8,128)(2,1)}, bf16[3,32,1024]{2,1,0:T(8,128)(2,1)S(1)}, u32[]{:S(2)}, u32[]{:S(2)}) %collective-permute-start.1) | collective-permute-done | bytes 196640 | tf_op jit(solution)/shard_map/ppermute | solution.py:18
  23.2 2.9 %concatenate.30 = bf16[4,4,24,2562]{3,2,0,1:T(8,128)(2,1)} concatenate(bf16[4,4,24,2048]{3,2,0,1:T(8,128)(2,1)S(1)} %copy.84, bf16[4,4,24,512]{3,2,0,1:T(8,128)(2,1)S(1)} %copy.85, bf16[4,4,24,1]{3,2,0,1:T(8,128)(2,1)S(1)} %copy.86, bf16[4,4,24,1]{3,2,0,1:T(8,128)(2,1)S(1)} %copy.87), dimensions={3} | concatenate | bytes 3935232 | tf_op jit(solution)/shard_map/concatenate | solution.py:120
  26.1 4.6 %all-to-all-start = ((bf16[4,4,24,2562]{3,2,1,0:T(8,128)(2,1)}), bf16[4,4,24,2562]{3,2,1,0:T(8,128)(2,1)S(1)}, u32[]{:S(2)}, u32[]{:S(2)}) async-start(bf16[4,4,24,2562]{3,2,1,0:T(8,128)(2,1)} %bitcast.178), calls=%async_computation | async-start | bytes 4128768 | tf_op jit(solution)/shard_map/all_to_all | solution.py:123
  32.8 23.0 %all-to-all-done = bf16[4,4,24,2562]{3,2,1,0:T(8,128)(2,1)S(1)} async-done(((bf16[4,4,24,2562]{3,2,1,0:T(8,128)(2,1)}), bf16[4,4,24,2562]{3,2,1,0:T(8,128)(2,1)S(1)}, u32[]{:S(2)}, u32[]{:S(2)}) %all-to-all-start) | async-done | bytes 1967648 | tf_op jit(solution)/shard_map/all_to_all | solution.py:123
  57.0 5.4 %all-to-all-start.1 = ((f32[4,24,2562]{2,1,0:T(8,128)}), f32[4,24,2562]{2,1,0:T(8,128)S(1)}, u32[]{:S(2)}, u32[]{:S(2)}) async-start(f32[4,24,2562]{2,1,0:T(8,128)} %convert_reduce_fusion.1), calls=%async_computation.1 | async-start | bytes 2064384 | tf_op jit(solution)/shard_map/all_to_all | solution.py:124
  62.5 12.9 %all-to-all-done.1 = f32[4,24,2562]{2,1,0:T(8,128)S(1)} async-done(((f32[4,24,2562]{2,1,0:T(8,128)}), f32[4,24,2562]{2,1,0:T(8,128)S(1)}, u32[]{:S(2)}, u32[]{:S(2)}) %all-to-all-start.1) | async-done | bytes 983840 | tf_op jit(solution)/shard_map/all_to_all | solution.py:124
  81.9 2.7 %collective-permute-done.4 = bf16[24,2048]{1,0:T(8,128)(2,1)S(1)} collective-permute-done((bf16[24,2048]{1,0:T(8,128)(2,1)S(1)}, bf16[24,2048]{1,0:T(8,128)(2,1)S(1)}, u32[]{:S(2)}, u32[]{:S(2)}) %collective-permute-start.4) | collective-permute-done | bytes 98336 | tf_op jit(solution)/shard_map/ppermute | solution.py:18
  90.5 7.8 %collective-permute-done.7 = bf16[4,24,2048]{2,1,0:T(8,128)(2,1)S(1)} collective-permute-done((bf16[4,24,2048]{2,1,0:T(8,128)(2,1)S(1)}, bf16[4,24,2048]{2,1,0:T(8,128)(2,1)S(1)}, u32[]{:S(2)}, u32[]{:S(2)}) %collective-permute-start.7) | collective-permute-done | bytes 393248 | tf_op jit(solution)/shard_map/ppermute | solution.py:18
  98.3 4.1 %collective-permute-done.6 = bf16[4,24,2048]{2,1,0:T(8,128)(2,1)S(1)} collective-permute-done((bf16[4,24,2048]{2,1,0:T(8,128)(2,1)S(1)}, bf16[4,24,2048]{2,1,0:T(8,128)(2,1)S(1)}, u32[]{:S(2)}, u32[]{:S(2)}) %collective-permute-start.6) | collective-permute-done | bytes 393248 | tf_op jit(solution)/shard_map/ppermute | solution.py:18
  107.0 2.7 %fusion.14 = bf16[384,1024]{1,0:T(8,128)(2,1)} fusion(bf16[384,2048]{1,0:T(8,128)(2,1)S(1)} %bitcast.183, bf16[1,2048,1024]{2,1,0:T(8,128)(2,1)S(1)} %copy-done.15), kind=kOutput, calls=%fused_computation.34 | convolution fusion | flops 1611005952 | bytes 6553600 | tf_op jit(solution)/shard_map/dot_general | solution.py:152
  109.7 4.5 %all-to-all-start.2 = ((bf16[4,96,1024]{2,1,0:T(8,128)(2,1)}), bf16[4,96,1024]{2,1,0:T(8,128)(2,1)}, u32[]{:S(2)}, u32[]{:S(2)}) async-start(bf16[4,96,1024]{2,1,0:T(8,128)(2,1)} %bitcast.38), calls=%async_computation.2 | async-start | bytes 1572864 | tf_op jit(solution)/shard_map/all_to_all | solution.py:162
  114.6 10.3 %all-to-all-done.2 = bf16[4,96,1024]{2,1,0:T(8,128)(2,1)} async-done(((bf16[4,96,1024]{2,1,0:T(8,128)(2,1)}), bf16[4,96,1024]{2,1,0:T(8,128)(2,1)}, u32[]{:S(2)}, u32[]{:S(2)}) %all-to-all-start.2) | async-done | bytes 786464 | tf_op jit(solution)/shard_map/all_to_all | solution.py:162
  129.0 3.1 %collective-permute-done.11 = bf16[96,1024]{1,0:T(8,128)(2,1)S(1)} collective-permute-done((bf16[96,1024]{1,0:T(8,128)(2,1)S(1)}, bf16[96,1024]{1,0:T(8,128)(2,1)S(1)}, u32[]{:S(2)}, u32[]{:S(2)}) %collective-permute-start.11) | collective-permute-done | bytes 196640 | tf_op jit(solution)/shard_map/ppermute | solution.py:18
  143.1 4.0 %fusion.11 = bf16[384,2048]{1,0:T(8,128)(2,1)S(1)} fusion(bf16[1,1024,2048]{2,1,0:T(8,128)(2,1)} %param.16, bf16[384,1024]{1,0:T(8,128)(2,1)S(1)} %collective-permute-done.12, f32[1024]{0:T(1024)S(1)} %bitcast.224), kind=kOutput, calls=%fused_computation.23 | convolution fusion | flops 1612578816 | bytes 6557696 | tf_op jit(solution)/shard_map/dot_general | solution.py:118
  147.2 2.9 %concatenate.35 = bf16[4,4,24,2562]{3,2,0,1:T(8,128)(2,1)} concatenate(bf16[4,4,24,2048]{3,2,0,1:T(8,128)(2,1)S(1)} %copy.95, bf16[4,4,24,512]{3,2,0,1:T(8,128)(2,1)S(1)} %copy.96, bf16[4,4,24,1]{3,2,0,1:T(8,128)(2,1)S(1)} %copy.97, bf16[4,4,24,1]{3,2,0,1:T(8,128)(2,1)S(1)} %copy.98), dimensions={3} | concatenate | bytes 3935232 | tf_op jit(solution)/shard_map/concatenate | solution.py:120
  150.1 3.7 %all-to-all-start.3 = ((bf16[4,4,24,2562]{3,2,1,0:T(8,128)(2,1)}), bf16[4,4,24,2562]{3,2,1,0:T(8,128)(2,1)S(1)}, u32[]{:S(2)}, u32[]{:S(2)}) async-start(bf16[4,4,24,2562]{3,2,1,0:T(8,128)(2,1)} %bitcast.179), calls=%async_computation.3 | async-start | bytes 4128768 | tf_op jit(solution)/shard_map/all_to_all | solution.py:123
  154.7 25.9 %all-to-all-done.3 = bf16[4,4,24,2562]{3,2,1,0:T(8,128)(2,1)S(1)} async-done(((bf16[4,4,24,2562]{3,2,1,0:T(8,128)(2,1)}), bf16[4,4,24,2562]{3,2,1,0:T(8,128)(2,1)S(1)}, u32[]{:S(2)}, u32[]{:S(2)}) %all-to-all-start.3) | async-done | bytes 1967648 | tf_op jit(solution)/shard_map/all_to_all | solution.py:123
  181.8 3.7 %all-to-all-start.4 = ((f32[4,24,2562]{2,1,0:T(8,128)}), f32[4,24,2562]{2,1,0:T(8,128)S(1)}, u32[]{:S(2)}, u32[]{:S(2)}) async-start(f32[4,24,2562]{2,1,0:T(8,128)} %convert_reduce_fusion), calls=%async_computation.4 | async-start | bytes 2064384 | tf_op jit(solution)/shard_map/all_to_all | solution.py:124
  186.0 14.2 %all-to-all-done.4 = f32[4,24,2562]{2,1,0:T(8,128)S(1)} async-done(((f32[4,24,2562]{2,1,0:T(8,128)}), f32[4,24,2562]{2,1,0:T(8,128)S(1)}, u32[]{:S(2)}, u32[]{:S(2)}) %all-to-all-start.4) | async-done | bytes 983840 | tf_op jit(solution)/shard_map/all_to_all | solution.py:124
  206.7 2.7 %collective-permute-done.14 = bf16[24,2048]{1,0:T(8,128)(2,1)S(1)} collective-permute-done((bf16[24,2048]{1,0:T(8,128)(2,1)S(1)}, bf16[24,2048]{1,0:T(8,128)(2,1)S(1)}, u32[]{:S(2)}, u32[]{:S(2)}) %collective-permute-start.14) | collective-permute-done | bytes 98336 | tf_op jit(solution)/shard_map/ppermute | solution.py:18
  215.3 9.5 %collective-permute-done.17 = bf16[4,24,2048]{2,1,0:T(8,128)(2,1)S(1)} collective-permute-done((bf16[4,24,2048]{2,1,0:T(8,128)(2,1)S(1)}, bf16[4,24,2048]{2,1,0:T(8,128)(2,1)S(1)}, u32[]{:S(2)}, u32[]{:S(2)}) %collective-permute-start.17) | collective-permute-done | bytes 393248 | tf_op jit(solution)/shard_map/ppermute | solution.py:18
  224.9 4.3 %collective-permute-done.16 = bf16[4,24,2048]{2,1,0:T(8,128)(2,1)S(1)} collective-permute-done((bf16[4,24,2048]{2,1,0:T(8,128)(2,1)S(1)}, bf16[4,24,2048]{2,1,0:T(8,128)(2,1)S(1)}, u32[]{:S(2)}, u32[]{:S(2)}) %collective-permute-start.16) | collective-permute-done | bytes 393248 | tf_op jit(solution)/shard_map/ppermute | solution.py:18
  238.9 3.5 %all-to-all-start.5 = ((bf16[4,3,32,1024]{3,2,1,0:T(8,128)(2,1)}), bf16[4,3,32,1024]{3,2,1,0:T(8,128)(2,1)S(1)}, u32[]{:S(2)}, u32[]{:S(2)}) async-start(bf16[4,3,32,1024]{3,2,1,0:T(8,128)(2,1)} %bitcast.174), calls=%async_computation.5 | async-start | bytes 1572864 | tf_op jit(solution)/shard_map/all_to_all | solution.py:157
  247.5 7.6 %all-to-all-done.5 = bf16[4,3,32,1024]{3,2,1,0:T(8,128)(2,1)S(1)} async-done(((bf16[4,3,32,1024]{3,2,1,0:T(8,128)(2,1)}), bf16[4,3,32,1024]{3,2,1,0:T(8,128)(2,1)S(1)}, u32[]{:S(2)}, u32[]{:S(2)}) %all-to-all-start.5) | async-done | bytes 786464 | tf_op jit(solution)/shard_map/all_to_all | solution.py:157
  (208 shorter events, 85.6 us)
Async XLA Ops:
  0.6 8.1 %collective-permute-start = (bf16[3,32,1024]{2,1,0:T(8,128)(2,1)}, bf16[3,32,1024]{2,1,0:T(8,128)(2,1)S(1)}, u32[]{:S(2)}, u32[]{:S(2)}) collective-permute-start(bf16[3,32,1024]{2,1,0:T(8,128)(2,1)} %param.14), channel_id=1, source_target_pairs={{0,16},{16,32},{32,48},{48,0},{1,17},{17,33},{33,49},{49,1},{2,18}... | collective-permute-start | bytes 589832 | tf_op jit(solution)/shard_map/ppermute | solution.py:18
  2.3 8.0 %collective-permute-start.2 = (bf16[3,32,1024]{2,1,0:T(8,128)(2,1)}, bf16[3,32,1024]{2,1,0:T(8,128)(2,1)S(1)}, u32[]{:S(2)}, u32[]{:S(2)}) collective-permute-start(bf16[3,32,1024]{2,1,0:T(8,128)(2,1)} %param.14), channel_id=1, source_target_pairs={{0,48},{16,0},{32,16},{48,32},{1,49},{17,1},{33,17},{49,33},{2,50}... | collective-permute-start | bytes 589832 | tf_op jit(solution)/shard_map/ppermute | solution.py:18
  4.0 10.1 %collective-permute-start.1 = (bf16[3,32,1024]{2,1,0:T(8,128)(2,1)}, bf16[3,32,1024]{2,1,0:T(8,128)(2,1)S(1)}, u32[]{:S(2)}, u32[]{:S(2)}) collective-permute-start(bf16[3,32,1024]{2,1,0:T(8,128)(2,1)} %param.14), channel_id=1, source_target_pairs={{0,32},{16,48},{32,0},{48,16},{1,33},{17,49},{33,1},{49,17},{2,34}... | collective-permute-start | bytes 589832 | tf_op jit(solution)/shard_map/ppermute | solution.py:18
  26.1 29.7 %all-to-all-start = ((bf16[4,4,24,2562]{3,2,1,0:T(8,128)(2,1)}), bf16[4,4,24,2562]{3,2,1,0:T(8,128)(2,1)S(1)}, u32[]{:S(2)}, u32[]{:S(2)}) async-start(bf16[4,4,24,2562]{3,2,1,0:T(8,128)(2,1)} %bitcast.178), calls=%async_computation | async-start | bytes 4128768 | tf_op jit(solution)/shard_map/all_to_all | solution.py:123
  57.0 18.4 %all-to-all-start.1 = ((f32[4,24,2562]{2,1,0:T(8,128)}), f32[4,24,2562]{2,1,0:T(8,128)S(1)}, u32[]{:S(2)}, u32[]{:S(2)}) async-start(f32[4,24,2562]{2,1,0:T(8,128)} %convert_reduce_fusion.1), calls=%async_computation.1 | async-start | bytes 2064384 | tf_op jit(solution)/shard_map/all_to_all | solution.py:124
  77.2 4.7 %collective-permute-start.5 = (bf16[24,2048]{1,0:T(8,128)(2,1)S(1)}, bf16[24,2048]{1,0:T(8,128)(2,1)S(1)}, u32[]{:S(2)}, u32[]{:S(2)}) collective-permute-start(bf16[24,2048]{1,0:T(8,128)(2,1)S(1)} %reshape.632), channel_id=1, source_target_pairs={{0,12},{4,0},{8,4},{12,8},{1,13},{5,1},{9,5},{13,9},{2,14},{6,2},{... | collective-permute-start | bytes 294920 | tf_op jit(solution)/shard_map/ppermute | solution.py:18
  78.4 6.1 %collective-permute-start.4 = (bf16[24,2048]{1,0:T(8,128)(2,1)S(1)}, bf16[24,2048]{1,0:T(8,128)(2,1)S(1)}, u32[]{:S(2)}, u32[]{:S(2)}) collective-permute-start(bf16[24,2048]{1,0:T(8,128)(2,1)S(1)} %reshape.632), channel_id=1, source_target_pairs={{0,8},{4,12},{8,0},{12,4},{1,9},{5,13},{9,1},{13,5},{2,10},{6,14},... | collective-permute-start | bytes 294920 | tf_op jit(solution)/shard_map/ppermute | solution.py:18
  79.9 5.8 %collective-permute-start.3 = (bf16[24,2048]{1,0:T(8,128)(2,1)S(1)}, bf16[24,2048]{1,0:T(8,128)(2,1)S(1)}, u32[]{:S(2)}, u32[]{:S(2)}) collective-permute-start(bf16[24,2048]{1,0:T(8,128)(2,1)S(1)} %reshape.632), channel_id=1, source_target_pairs={{0,4},{4,8},{8,12},{12,0},{1,5},{5,9},{9,13},{13,1},{2,6},{6,10},{... | collective-permute-start | bytes 294920 | tf_op jit(solution)/shard_map/ppermute | solution.py:18
  86.5 11.8 %collective-permute-start.7 = (bf16[4,24,2048]{2,1,0:T(8,128)(2,1)S(1)}, bf16[4,24,2048]{2,1,0:T(8,128)(2,1)S(1)}, u32[]{:S(2)}, u32[]{:S(2)}) collective-permute-start(bf16[4,24,2048]{2,1,0:T(8,128)(2,1)S(1)} %broadcast_select_fusion.2), channel_id=1, source_target_pairs={{0,2},{1,3},{2,0},{3,1},{4,6},{5,7},{6,4},{7,5},{8,10},{9,11},{10,... | collective-permute-start | bytes 1179656 | tf_op jit(solution)/shard_map/ppermute | solution.py:18
  87.2 15.2 %collective-permute-start.6 = (bf16[4,24,2048]{2,1,0:T(8,128)(2,1)S(1)}, bf16[4,24,2048]{2,1,0:T(8,128)(2,1)S(1)}, u32[]{:S(2)}, u32[]{:S(2)}) collective-permute-start(bf16[4,24,2048]{2,1,0:T(8,128)(2,1)S(1)} %broadcast_select_fusion.2), channel_id=1, source_target_pairs={{0,1},{1,2},{2,3},{3,0},{4,5},{5,6},{6,7},{7,4},{8,9},{9,10},{10,1... | collective-permute-start | bytes 1179656 | tf_op jit(solution)/shard_map/ppermute | solution.py:18
  88.6 13.8 %collective-permute-start.8 = (bf16[4,24,2048]{2,1,0:T(8,128)(2,1)S(1)}, bf16[4,24,2048]{2,1,0:T(8,128)(2,1)S(1)}, u32[]{:S(2)}, u32[]{:S(2)}) collective-permute-start(bf16[4,24,2048]{2,1,0:T(8,128)(2,1)S(1)} %broadcast_select_fusion.2), channel_id=1, source_target_pairs={{0,3},{1,0},{2,1},{3,2},{4,7},{5,4},{6,5},{7,6},{8,11},{9,8},{10,9... | collective-permute-start | bytes 1179656 | tf_op jit(solution)/shard_map/ppermute | solution.py:18
  109.7 15.2 %all-to-all-start.2 = ((bf16[4,96,1024]{2,1,0:T(8,128)(2,1)}), bf16[4,96,1024]{2,1,0:T(8,128)(2,1)}, u32[]{:S(2)}, u32[]{:S(2)}) async-start(bf16[4,96,1024]{2,1,0:T(8,128)(2,1)} %bitcast.38), calls=%async_computation.2 | async-start | bytes 1572864 | tf_op jit(solution)/shard_map/all_to_all | solution.py:162
  126.3 5.9 %collective-permute-start.11 = (bf16[96,1024]{1,0:T(8,128)(2,1)S(1)}, bf16[96,1024]{1,0:T(8,128)(2,1)S(1)}, u32[]{:S(2)}, u32[]{:S(2)}) collective-permute-start(bf16[96,1024]{1,0:T(8,128)(2,1)S(1)} %fusion.35), channel_id=1, source_target_pairs={{0,48},{16,0},{32,16},{48,32},{1,49},{17,1},{33,17},{49,33},{2,50}... | collective-permute-start | bytes 589832 | tf_op jit(solution)/shard_map/ppermute | solution.py:18
  127.5 7.3 %collective-permute-start.10 = (bf16[96,1024]{1,0:T(8,128)(2,1)S(1)}, bf16[96,1024]{1,0:T(8,128)(2,1)S(1)}, u32[]{:S(2)}, u32[]{:S(2)}) collective-permute-start(bf16[96,1024]{1,0:T(8,128)(2,1)S(1)} %fusion.35), channel_id=1, source_target_pairs={{0,32},{16,48},{32,0},{48,16},{1,33},{17,49},{33,1},{49,17},{2,34}... | collective-permute-start | bytes 589832 | tf_op jit(solution)/shard_map/ppermute | solution.py:18
  129.0 7.8 %collective-permute-start.9 = (bf16[96,1024]{1,0:T(8,128)(2,1)S(1)}, bf16[96,1024]{1,0:T(8,128)(2,1)S(1)}, u32[]{:S(2)}, u32[]{:S(2)}) collective-permute-start(bf16[96,1024]{1,0:T(8,128)(2,1)S(1)} %fusion.35), channel_id=1, source_target_pairs={{0,16},{16,32},{32,48},{48,0},{1,17},{17,33},{33,49},{49,1},{2,18}... | collective-permute-start | bytes 589832 | tf_op jit(solution)/shard_map/ppermute | solution.py:18
  150.1 30.5 %all-to-all-start.3 = ((bf16[4,4,24,2562]{3,2,1,0:T(8,128)(2,1)}), bf16[4,4,24,2562]{3,2,1,0:T(8,128)(2,1)S(1)}, u32[]{:S(2)}, u32[]{:S(2)}) async-start(bf16[4,4,24,2562]{3,2,1,0:T(8,128)(2,1)} %bitcast.179), calls=%async_computation.3 | async-start | bytes 4128768 | tf_op jit(solution)/shard_map/all_to_all | solution.py:123
  181.8 18.4 %all-to-all-start.4 = ((f32[4,24,2562]{2,1,0:T(8,128)}), f32[4,24,2562]{2,1,0:T(8,128)S(1)}, u32[]{:S(2)}, u32[]{:S(2)}) async-start(f32[4,24,2562]{2,1,0:T(8,128)} %convert_reduce_fusion), calls=%async_computation.4 | async-start | bytes 2064384 | tf_op jit(solution)/shard_map/all_to_all | solution.py:124
  202.0 4.7 %collective-permute-start.15 = (bf16[24,2048]{1,0:T(8,128)(2,1)S(1)}, bf16[24,2048]{1,0:T(8,128)(2,1)S(1)}, u32[]{:S(2)}, u32[]{:S(2)}) collective-permute-start(bf16[24,2048]{1,0:T(8,128)(2,1)S(1)} %reshape.637), channel_id=1, source_target_pairs={{0,12},{4,0},{8,4},{12,8},{1,13},{5,1},{9,5},{13,9},{2,14},{6,2},{... | collective-permute-start | bytes 294920 | tf_op jit(solution)/shard_map/ppermute | solution.py:18
  203.2 6.1 %collective-permute-start.14 = (bf16[24,2048]{1,0:T(8,128)(2,1)S(1)}, bf16[24,2048]{1,0:T(8,128)(2,1)S(1)}, u32[]{:S(2)}, u32[]{:S(2)}) collective-permute-start(bf16[24,2048]{1,0:T(8,128)(2,1)S(1)} %reshape.637), channel_id=1, source_target_pairs={{0,8},{4,12},{8,0},{12,4},{1,9},{5,13},{9,1},{13,5},{2,10},{6,14},... | collective-permute-start | bytes 294920 | tf_op jit(solution)/shard_map/ppermute | solution.py:18
  204.7 5.8 %collective-permute-start.13 = (bf16[24,2048]{1,0:T(8,128)(2,1)S(1)}, bf16[24,2048]{1,0:T(8,128)(2,1)S(1)}, u32[]{:S(2)}, u32[]{:S(2)}) collective-permute-start(bf16[24,2048]{1,0:T(8,128)(2,1)S(1)} %reshape.637), channel_id=1, source_target_pairs={{0,4},{4,8},{8,12},{12,0},{1,5},{5,9},{9,13},{13,1},{2,6},{6,10},{... | collective-permute-start | bytes 294920 | tf_op jit(solution)/shard_map/ppermute | solution.py:18
  211.3 13.6 %collective-permute-start.17 = (bf16[4,24,2048]{2,1,0:T(8,128)(2,1)S(1)}, bf16[4,24,2048]{2,1,0:T(8,128)(2,1)S(1)}, u32[]{:S(2)}, u32[]{:S(2)}) collective-permute-start(bf16[4,24,2048]{2,1,0:T(8,128)(2,1)S(1)} %broadcast_select_fusion.1), channel_id=1, source_target_pairs={{0,2},{1,3},{2,0},{3,1},{4,6},{5,7},{6,4},{7,5},{8,10},{9,11},{10,... | collective-permute-start | bytes 1179656 | tf_op jit(solution)/shard_map/ppermute | solution.py:18
  212.0 17.2 %collective-permute-start.16 = (bf16[4,24,2048]{2,1,0:T(8,128)(2,1)S(1)}, bf16[4,24,2048]{2,1,0:T(8,128)(2,1)S(1)}, u32[]{:S(2)}, u32[]{:S(2)}) collective-permute-start(bf16[4,24,2048]{2,1,0:T(8,128)(2,1)S(1)} %broadcast_select_fusion.1), channel_id=1, source_target_pairs={{0,1},{1,2},{2,3},{3,0},{4,5},{5,6},{6,7},{7,4},{8,9},{9,10},{10,1... | collective-permute-start | bytes 1179656 | tf_op jit(solution)/shard_map/ppermute | solution.py:18
  213.4 15.8 %collective-permute-start.18 = (bf16[4,24,2048]{2,1,0:T(8,128)(2,1)S(1)}, bf16[4,24,2048]{2,1,0:T(8,128)(2,1)S(1)}, u32[]{:S(2)}, u32[]{:S(2)}) collective-permute-start(bf16[4,24,2048]{2,1,0:T(8,128)(2,1)S(1)} %broadcast_select_fusion.1), channel_id=1, source_target_pairs={{0,3},{1,0},{2,1},{3,2},{4,7},{5,4},{6,5},{7,6},{8,11},{9,8},{10,9... | collective-permute-start | bytes 1179656 | tf_op jit(solution)/shard_map/ppermute | solution.py:18
  238.9 16.2 %all-to-all-start.5 = ((bf16[4,3,32,1024]{3,2,1,0:T(8,128)(2,1)}), bf16[4,3,32,1024]{3,2,1,0:T(8,128)(2,1)S(1)}, u32[]{:S(2)}, u32[]{:S(2)}) async-start(bf16[4,3,32,1024]{3,2,1,0:T(8,128)(2,1)} %bitcast.174), calls=%async_computation.5 | async-start | bytes 1572864 | tf_op jit(solution)/shard_map/all_to_all | solution.py:157
  (18 other events, 150.3 us)
